TPU v7x, 256 devices: a whole 4x4x8 slice. The times are simulated.
256 devices in a mesh: grp: 8 (over y_hi, x), dom: 32 (over y_lo, z, core).
Axes of the slice: x: 4, y: 4 (y_hi: 2, y_lo: 2; y = y_hi * 2 + y_lo), z: 8, core: 2. Of those that a mesh axis runs over, the one named last changes fastest.
Arguments:
- fine_matrix_blocks: bfloat16 [16384, 64, 768], P(('grp', 'dom')), may hold values from -0.21875 to 0.21875
- prolongator: bfloat16 [16384, 64, 64], P(('grp', 'dom')), may hold values from -1.5 to 1.5
- block_columns: int32 [16384, 12], P(('grp', 'dom')), may hold values from 0 to 16383, as said below
- block_aggregates: int32 [16384, 12], P(('grp', 'dom')), may hold values from 0 to 1023, as said below
- live_counts: int32 [256], P(('grp', 'dom')), may hold values from 16 to 64, as said below
Outputs:
- coarse_operator: float32 [1024, 64, 768], P('dom')
Inputs may be any that keep to these rules, and one draw needn't show every extreme that they name: live_counts[p] counts the first slots of partition p that hold block rows; some partition has 64 and some has 16. `block_columns`: entry 0 of row i is i itself. For a live row of partition p, every entry is a live row of partition p - 1, p or p + 1 (only partitions that exist); entries may repeat, and repeated blocks add. block_aggregates[i, k] is the aggregate of row block_columns[i, k]. Every row of partition p, with g = p // 32 and q = p % 32, has an aggregate from (((q + 4 * g) % 32) * 8 + g) * 4 to that number plus 4 - 1.
All inputs are finite; a program needn't handle non-finite values.
Results may differ from a plain program's by a relative error of at most 0.0029.
Values may be sent and summed in bfloat16 or wider, within the bound.
No kernel may reach another device: no remote copies, remote signals or barrier semaphores. Data moves between devices by JAX's collectives and lax.ppermute only.
A program may use at most 192 MiB of HBM per device.

v0:
```python
import jax
import jax.numpy as jnp
from jax import lax
from jax.sharding import PartitionSpec as P

AGG_DEV = 4


def extended(block, sides, width):
    for axis, dim in sides:
        count = lax.axis_size(axis)
        forward = [(i, i + 1) for i in range(count - 1)]
        backward = [(target, source) for source, target in forward]
        low = lax.ppermute(
            lax.slice_in_dim(block, block.shape[dim] - width, None, axis=dim), axis, forward
        )
        high = lax.ppermute(lax.slice_in_dim(block, 0, width, axis=dim), axis, backward)
        block = jnp.concatenate([low, block, high], axis=dim)
    return block


def passed_along(value, axis, by):
    peers = lax.axis_size(axis)
    return lax.ppermute(value, axis, [(i, (i + by) % peers) for i in range(peers)])


def local(fine_matrix_blocks, prolongator, block_columns, block_aggregates, live_counts):
    capacity = fine_matrix_blocks.shape[0]
    block_width = prolongator.shape[1]
    row_blocks = block_columns.shape[1]
    slot_width = 3 * AGG_DEV
    position = lax.axis_index(("grp", "dom"))
    ghosts = extended(prolongator, ((("grp", "dom"), 0),), capacity)
    local_rows = block_columns - (position - 1) * capacity
    gathered = jnp.take(ghosts, local_rows, axis=0)
    matrix_view = fine_matrix_blocks.reshape(capacity, block_width, row_blocks, block_width)
    products = jnp.einsum(
        "ixky,ikyz->ixkz", matrix_view, gathered, preferred_element_type=jnp.float32
    )
    coarse_slot = AGG_DEV * (local_rows // capacity) + block_aggregates % AGG_DEV
    live_rows = jnp.arange(capacity) < live_counts[0]
    slot_select = (coarse_slot[:, :, None] == jnp.arange(slot_width)[None, None, :]) & live_rows[
        :, None, None
    ]
    row_sums = jnp.einsum(
        "ikt,ixkz->ixtz", slot_select.astype(jnp.float32), products, precision=lax.Precision.HIGHEST
    )
    row_sums = row_sums.astype(jnp.bfloat16).reshape(
        capacity * block_width, slot_width * block_width
    )
    row_select = (block_aggregates[:, 0:1] % AGG_DEV == jnp.arange(AGG_DEV)[None, :]) & live_rows[
        :, None
    ]
    spread = row_select.astype(jnp.bfloat16)[:, None, :, None] * prolongator[:, :, None, :]
    spread = spread.reshape(capacity * block_width, AGG_DEV * block_width)
    coarse = lax.dot_general(
        spread, row_sums, (((0,), (0,)), ((), ())), preferred_element_type=jnp.float32
    )
    groups_count = lax.axis_size("grp")
    step_stride = lax.axis_size("dom") // groups_count
    group_index = lax.axis_index("grp")
    rotated = coarse
    for bit_number in range(groups_count.bit_length() - 1):
        arrived = passed_along(rotated, "dom", step_stride << bit_number)
        rotated = jnp.where((group_index >> bit_number) % 2 == 1, arrived, rotated)
    result = lax.all_gather(rotated[None], "grp", axis=0, tiled=True)
    return result.reshape(groups_count * AGG_DEV, block_width, slot_width * block_width)


def solution(mesh):
    return jax.shard_map(
        local,
        mesh=mesh,
        in_specs=(
            P(("grp", "dom"), None, None),
            P(("grp", "dom"), None, None),
            P(("grp", "dom"), None),
            P(("grp", "dom"), None),
            P(("grp", "dom")),
        ),
        out_specs=P("dom", None, None),
        check_vma=False,
    )
```

profile of v0, /device:TPU:96, one launch (start us, length us, event | category | flops | bytes accessed | tf_op | source)
XLA Modules:
  0.0 394.2 jit_solution(863986176305773852)
XLA Ops:
  6.5 0.0 copy-start.1
  6.5 0.0 all-gather.3.cloned.1.call-start
  6.5 2.0 collective-permute-start
  8.6 3.6 collective-permute-start.1
  12.3 0.7 compare_and_fusion
  13.0 0.7 fusion.17
  13.7 0.7 fusion.22
  14.4 0.1 copy.14
  14.5 0.1 reshape.79
  14.6 0.1 copy.13
  14.7 19.7 %reshape.74 = bf16[64,64,12,64]{3,2,1,0:T(8,128)(2,1)} reshape(bf16[64,64,768]{2,1,0:T(8,128)(2,1)} %param.5) | data formatting | bytes 12582912 | tf_op jit(solution)/shard_map/reshape | solution.py:36
  34.4 0.1 copy.17
  35.2 0.1 copy.12
  35.3 0.0 copy-done.1
  35.3 4.2 %broadcast_multiply_fusion = bf16[64,64,4,64]{3,2,1,0:T(4,128)(2,1)} fusion(bf16[64,64,64]{2,1,0:T(8,128)(2,1)S(1)} %copy-done.1, bf16[64,4]{1,0:T(8,128)(2,1)S(1)} %copy.12), kind=kLoop, calls=%fused_computation.9 | loop fusion | flops 1048576 | bytes 2621952 | tf_op jit(solution)/shard_map/mul | solution.py:54
  39.5 7.0 %mul.38 = bf16[4096,256]{1,0:T(8,128)(2,1)} reshape(bf16[64,64,4,64]{3,2,1,0:T(4,128)(2,1)} %broadcast_multiply_fusion) | data formatting | bytes 4194304 | tf_op jit(solution)/shard_map/mul | solution.py:54
  46.5 0.0 collective-permute-done
  46.5 0.0 copy-start.2
  46.5 1.0 copy-done.2
  47.4 0.0 collective-permute-done.1
  47.4 2.2 pad_maximum_fusion
  49.7 18.2 %gather_fusion = bf16[768,64,64]{2,1,0:T(8,128)(2,1)} fusion(bf16[192,64,64]{2,1,0:T(8,128)(2,1)S(1)} %pad_maximum_fusion, s32[1024]{0:T(1024)S(1)} %pad_clamp_fusion), kind=kCustom, calls=%fused_computation | custom fusion | bytes 12585984 | tf_op jit(solution)/shard_map/jit(_take)/gather | solution.py:35
  67.8 16.6 %copy.15 = bf16[64,12,64,64]{2,3,1,0:T(8,128)(2,1)} copy(bf16[64,12,64,64]{3,2,1,0:T(8,128)(2,1)} %bitcast.18) | data formatting | bytes 12582912 | tf_op jit(solution)/shard_map/jit(_take)/gather | solution.py:35
  84.5 21.7 %fusion.4 = f32[64,64,12,64]{1,3,2,0:T(8,128)} fusion(bf16[64,64,12,64]{3,2,1,0:T(8,128)(2,1)} %reshape.74, bf16[64,12,64,64]{2,3,1,0:T(8,128)(2,1)} %copy.15, pred[64,12]{1,0:T(8,128)(4,1)S(1)} %copy.13), kind=kOutput, calls=%fused_computation.6 | convolution fusion | flops 405798912 | bytes 25166592 | tf_op jit(solution)/shard_map/ixky,ikyz->ixkz/dot_general | solution.py:37
  106.2 31.1 %copy.18 = f32[64,64,12,64]{3,2,1,0:T(8,128)} copy(f32[64,64,12,64]{1,3,2,0:T(8,128)} %fusion.4) | data formatting | bytes 25165824 | tf_op jit(solution)/shard_map/ixky,ikyz->ixkz/transpose | solution.py:37
  137.3 25.0 %convert_bitcast_fusion = bf16[64,64,12,64]{3,2,1,0:T(8,128)(2,1)} fusion(f32[64,64,12,64]{3,2,1,0:T(8,128)} %copy.18, s32[64,12]{1,0:T(8,128)S(1)} %copy.17, pred[64]{0:T(512)(128)(4,1)S(1)} %iota_compare_fusion.2), kind=kOutput, calls=%fused_computation.1 | convolution fusion | flops 456148992 | bytes 18877504 | tf_op jit(solution)/shard_map/ikt,ixkz->ixtz/dot_general | solution.py:45
  162.3 0.0 copy-start
  162.3 20.9 %reshape.90 = bf16[4096,768]{1,0:T(8,128)(2,1)} reshape(bf16[64,64,12,64]{3,2,1,0:T(8,128)(2,1)} %convert_bitcast_fusion) | data formatting | bytes 12582912 | tf_op jit(solution)/shard_map/reshape | solution.py:48
  183.2 0.0 copy-done
  183.2 4.6 %fusion.25 = f32[256,768]{1,0:T(8,128)S(1)} fusion(bf16[4096,256]{1,0:T(8,128)(2,1)S(1)} %copy-done, bf16[4096,768]{1,0:T(8,128)(2,1)} %reshape.90), kind=kOutput, calls=%fused_computation.44 | convolution fusion | flops 1610612736 | bytes 9175040 | tf_op jit(solution)/shard_map/dot_general | solution.py:56
  187.8 3.9 collective-permute-start.2
  191.7 33.7 %collective-permute-done.2 = f32[256,768]{1,0:T(8,128)S(1)} collective-permute-done((f32[256,768]{1,0:T(8,128)S(1)}, f32[256,768]{1,0:T(8,128)S(1)}, u32[]{:S(2)}, u32[]{:S(2)}) %collective-permute-start.2) | collective-permute-done | bytes 786464 | tf_op jit(solution)/shard_map/ppermute | solution.py:24
  225.3 0.1 broadcast_select_fusion
  225.4 3.5 collective-permute-start.3
  229.0 37.2 %collective-permute-done.3 = f32[256,768]{1,0:T(8,128)S(1)} collective-permute-done((f32[256,768]{1,0:T(8,128)S(1)}, f32[256,768]{1,0:T(8,128)S(1)}, u32[]{:S(2)}, u32[]{:S(2)}) %collective-permute-start.3) | collective-permute-done | bytes 786464 | tf_op jit(solution)/shard_map/ppermute | solution.py:24
  266.2 0.1 broadcast_select_fusion.1
  266.3 0.1 collective-permute-start.4
  266.4 19.2 %collective-permute-done.4 = f32[256,768]{1,0:T(8,128)S(1)} collective-permute-done((f32[256,768]{1,0:T(8,128)S(1)}, f32[256,768]{1,0:T(8,128)S(1)}, u32[]{:S(2)}, u32[]{:S(2)}) %collective-permute-start.4) | collective-permute-done | bytes 786464 | tf_op jit(solution)/shard_map/ppermute | solution.py:24
  285.6 1.0 broadcast_select_fusion.2
  286.6 0.0 all-gather.3.cloned.1.call-update
  286.6 94.7 %all-gather.3.cloned.1.call-done = f32[2048,768]{1,0:T(8,128)} async-done(((f32[256,768]{1,0:T(8,128)}), f32[2048,768]{1,0:T(8,128)}) %all-gather.3.cloned.1.call-update) | async-done | bytes 6291472 | tf_op jit(solution)/shard_map/all_gather | solution.py:66
  381.2 6.2 %copy.28 = f32[32,64,768]{2,1,0:T(8,128)} copy(f32[32,64,768]{2,1,0:T(8,128)} %bitcast.19) | data formatting | bytes 12582912
  (3 shorter events, 0.0 us)
Async XLA Ops:
  6.5 28.7 %copy-start.1 = (bf16[64,64,64]{2,1,0:T(8,128)(2,1)S(1)}, bf16[64,64,64]{2,1,0:T(8,128)(2,1)}, u32[]{:S(2)}) copy-start(bf16[64,64,64]{2,1,0:T(8,128)(2,1)} %param.6) | copy-start | bytes 1572868
  6.5 374.7 %all-gather.3.cloned.1.call-start = ((), (), s32[]{:S(2)}) async-start(), calls=%async_computation | async-start | bytes 7077888 | tf_op jit(solution)/shard_map/all_gather | solution.py:66
  6.5 39.9 %collective-permute-start = (bf16[64,64,64]{2,1,0:T(8,128)(2,1)}, bf16[64,64,64]{2,1,0:T(8,128)(2,1)S(1)}, u32[]{:S(2)}, u32[]{:S(2)}) collective-permute-start(bf16[64,64,64]{2,1,0:T(8,128)(2,1)} %param.6), channel_id=1, source_target_pairs={{0,1},{1,2},{2,3},{3,4},{4,5},{5,6},{6,7},{7,8},{8,9},{9,10},{10,1... | collective-permute-start | bytes 1572872 | tf_op jit(solution)/shard_map/ppermute | solution.py:14
  8.6 38.9 %collective-permute-start.1 = (bf16[64,64,64]{2,1,0:T(8,128)(2,1)}, bf16[64,64,64]{2,1,0:T(8,128)(2,1)}, u32[]{:S(2)}, u32[]{:S(2)}) collective-permute-start(bf16[64,64,64]{2,1,0:T(8,128)(2,1)} %param.6), channel_id=1, source_target_pairs={{1,0},{2,1},{3,2},{4,3},{5,4},{6,5},{7,6},{8,7},{9,8},{10,9},{11,1... | collective-permute-start | bytes 1572872 | tf_op jit(solution)/shard_map/ppermute | solution.py:17
  46.5 1.0 copy-start.2
  162.3 20.9 %copy-start = (bf16[4096,256]{1,0:T(8,128)(2,1)S(1)}, bf16[4096,256]{1,0:T(8,128)(2,1)}, u32[]{:S(2)}) copy-start(bf16[4096,256]{1,0:T(8,128)(2,1)} %mul.38) | copy-start | bytes 6291460
  187.8 37.6 %collective-permute-start.2 = (f32[256,768]{1,0:T(8,128)S(1)}, f32[256,768]{1,0:T(8,128)S(1)}, u32[]{:S(2)}, u32[]{:S(2)}) collective-permute-start(f32[256,768]{1,0:T(8,128)S(1)} %fusion.25), channel_id=1, source_target_pairs={{0,4},{1,5},{2,6},{3,7},{4,8},{5,9},{6,10},{7,11},{8,12},{9,13},{1... | collective-permute-start | bytes 2359304 | tf_op jit(solution)/shard_map/ppermute | solution.py:24
  225.4 40.7 %collective-permute-start.3 = (f32[256,768]{1,0:T(8,128)S(1)}, f32[256,768]{1,0:T(8,128)S(1)}, u32[]{:S(2)}, u32[]{:S(2)}) collective-permute-start(f32[256,768]{1,0:T(8,128)S(1)} %broadcast_select_fusion), channel_id=1, source_target_pairs={{0,8},{1,9},{2,10},{3,11},{4,12},{5,13},{6,14},{7,15},{8,16},{9,17... | collective-permute-start | bytes 2359304 | tf_op jit(solution)/shard_map/ppermute | solution.py:24
  266.3 19.3 %collective-permute-start.4 = (f32[256,768]{1,0:T(8,128)S(1)}, f32[256,768]{1,0:T(8,128)S(1)}, u32[]{:S(2)}, u32[]{:S(2)}) collective-permute-start(f32[256,768]{1,0:T(8,128)S(1)} %broadcast_select_fusion.1), channel_id=1, source_target_pairs={{0,16},{1,17},{2,18},{3,19},{4,20},{5,21},{6,22},{7,23},{8,24},{9,... | collective-permute-start | bytes 2359304 | tf_op jit(solution)/shard_map/ppermute | solution.py:24
Sparse Core Ops, SparseCore 0:
  286.7 94.4 all-gather.2
where the time goes:
time: 398 us; the launch traced here: 394 us
  waiting for transfers between devices  185 us (46%)
  local copies, waits for them, and re-layouts  121 us (30%)
  matrix products  51.3 us (13%)
  between operations  14.2 us (4%)
  starting transfers between devices  13.2 us (3%)
  other arithmetic  9.74 us (2%)
    all_gather x1, waiting for transfers between devices, local(): result = lax.all_gather(rotated[None], 'grp', axis=0, tiled=True)  94.7 us
    ppermute x3, waiting for transfers between devices, passed_along(): lax.ppermute(value, axis, [(i, (i + by) % peers) for i in range(peers)])  90.1 us
    gather x2, local copies, waits for them, and re-layouts, local(): gathered = jnp.take(ghosts, local_rows, axis=0)  34.8 us
    transpose x1, local copies, waits for them, and re-layouts, local(): jnp.einsum('ixky,ikyz->ixkz', matrix_view, gathered, preferred_element_ty...  31.1 us
    dot_general x1, matrix products, local(): jnp.einsum('ikt,ixkz->ixtz', slot_select.astype(jnp.float32), products, p...  25 us
    dot_general x1, matrix products, local(): jnp.einsum('ixky,ikyz->ixkz', matrix_view, gathered, preferred_element_ty...  21.7 us
    reshape x1, local copies, waits for them, and re-layouts, local(): row_sums.astype(jnp.bfloat16)  20.9 us
    reshape x1, local copies, waits for them, and re-layouts, local(): fine_matrix_blocks.reshape(capacity, block_width, row_blocks, block_width)  19.7 us
  transfers between devices with their start and end apart: 6, of which 4 were waited for; matrix products, arithmetic and copies ran while one was open for 9% of the time, Pallas kernels for 0%

commit v1 on v0

--- a/solution.py
+++ b/solution.py
@@ -17,11 +17,6 @@
         high = lax.ppermute(lax.slice_in_dim(block, 0, width, axis=dim), axis, backward)
         block = jnp.concatenate([low, block, high], axis=dim)
     return block
-
-
-def passed_along(value, axis, by):
-    peers = lax.axis_size(axis)
-    return lax.ppermute(value, axis, [(i, (i + by) % peers) for i in range(peers)])
 
 
 def local(fine_matrix_blocks, prolongator, block_columns, block_aggregates, live_counts):
@@ -57,13 +52,16 @@
         spread, row_sums, (((0,), (0,)), ((), ())), preferred_element_type=jnp.float32
     )
     groups_count = lax.axis_size("grp")
-    step_stride = lax.axis_size("dom") // groups_count
-    group_index = lax.axis_index("grp")
-    rotated = coarse
-    for bit_number in range(groups_count.bit_length() - 1):
-        arrived = passed_along(rotated, "dom", step_stride << bit_number)
-        rotated = jnp.where((group_index >> bit_number) % 2 == 1, arrived, rotated)
+    places = lax.axis_size("dom")
+    step_stride = places // groups_count
+    pairs = [
+        (g * places + q, g * places + (q + step_stride * g) % places)
+        for g in range(groups_count)
+        for q in range(places)
+    ]
+    rotated = lax.ppermute(coarse.astype(jnp.bfloat16), ("grp", "dom"), pairs)
     result = lax.all_gather(rotated[None], "grp", axis=0, tiled=True)
+    result = result.astype(jnp.float32)
     return result.reshape(groups_count * AGG_DEV, block_width, slot_width * block_width)
 
 

time: 398 us -> 300 us (0.75)
  waiting for transfers between devices: 185 us -> 94.7 us
  starting transfers between devices: 13.2 us -> 6.38 us
  local copies, waits for them, and re-layouts: 121 us -> 116 us
  other arithmetic: 9.74 us -> 14 us
    ppermute x3 -> x1, waiting for transfers between devices: 90.1 us -> 0.01 us  [local(): rotated = lax.ppermute(coarse.astype(jnp.bfloat16), ('grp', 'dom'), pairs)]
    ppermute x3 -> x1, starting transfers between devices: 7.51 us -> 0.69 us  [local(): rotated = lax.ppermute(coarse.astype(jnp.bfloat16), ('grp', 'dom'), pairs)]
    unnamed x7 -> x8, local copies, waits for them, and re-layouts: 7.15 us -> 1.71 us
    reshape x0 -> x1, other arithmetic: none -> 5.38 us  [local(): result.reshape(groups_count * AGG_DEV, block_width, slot_width * block_wi...]
  transfers between devices with their start and end apart: 6 -> 4, of which waited for: 4 -> 1; matrix products, arithmetic and copies ran while one was open for 9% -> 11% of each run, Pallas kernels for 0% -> 0%
where the time goes in v1:
time: 300 us; the launch traced here: 296 us
  local copies, waits for them, and re-layouts  116 us (39%)
  waiting for transfers between devices  94.7 us (32%)
  matrix products  51.3 us (17%)
  between operations  14.1 us (5%)
  other arithmetic  14 us (5%)
  starting transfers between devices  6.38 us (2%)
    all_gather x1, waiting for transfers between devices, local(): result = lax.all_gather(rotated[None], 'grp', axis=0, tiled=True)  94.7 us
    gather x2, local copies, waits for them, and re-layouts, local(): gathered = jnp.take(ghosts, local_rows, axis=0)  34.8 us
    transpose x1, local copies, waits for them, and re-layouts, local(): jnp.einsum('ixky,ikyz->ixkz', matrix_view, gathered, preferred_element_ty...  31.1 us
    dot_general x1, matrix products, local(): jnp.einsum('ikt,ixkz->ixtz', slot_select.astype(jnp.float32), products, p...  25 us
    dot_general x1, matrix products, local(): jnp.einsum('ixky,ikyz->ixkz', matrix_view, gathered, preferred_element_ty...  21.7 us
    reshape x1, local copies, waits for them, and re-layouts, local(): row_sums.astype(jnp.bfloat16)  20.9 us
    reshape x1, local copies, waits for them, and re-layouts, local(): fine_matrix_blocks.reshape(capacity, block_width, row_blocks, block_width)  19.7 us
    mul x1, local copies, waits for them, and re-layouts, local(): row_select.astype(jnp.bfloat16)[:, None, :, None]  6.95 us
  transfers between devices with their start and end apart: 4, of which 1 were waited for; matrix products, arithmetic and copies ran while one was open for 11% of the time, Pallas kernels for 0%

profile of v1, /device:TPU:96, one launch (start us, length us, event | category | flops | bytes accessed | tf_op | source)
XLA Modules:
  0.0 296.2 jit_solution(7769409100965928986)
XLA Ops:
  6.5 0.0 copy-start.1
  6.5 0.0 all-gather.3.cloned.1.call-start
  6.5 2.0 collective-permute-start
  8.6 3.6 %collective-permute-start.1 = (bf16[64,64,64]{2,1,0:T(8,128)(2,1)}, bf16[64,64,64]{2,1,0:T(8,128)(2,1)}, u32[]{:S(2)}, u32[]{:S(2)}) collective-permute-start(bf16[64,64,64]{2,1,0:T(8,128)(2,1)} %param.6), channel_id=1, source_target_pairs={{1,0},{2,1},{3,2},{4,3},{5,4},{6,5},{7,6},{8,7},{9,8},{10,9},{11,1... | collective-permute-start | bytes 1572872 | tf_op jit(solution)/shard_map/ppermute | solution.py:17
  12.2 0.7 compare_and_fusion
  13.0 0.7 fusion.17
  13.7 0.7 fusion.22
  14.4 0.1 copy.14
  14.5 0.1 reshape.85
  14.6 0.1 copy.13
  14.7 19.7 %reshape.77 = bf16[64,64,12,64]{3,2,1,0:T(8,128)(2,1)} reshape(bf16[64,64,768]{2,1,0:T(8,128)(2,1)} %param.5) | data formatting | bytes 12582912 | tf_op jit(solution)/shard_map/reshape | solution.py:31
  34.4 0.1 copy.17
  35.2 0.1 copy.12
  35.3 0.0 copy-done.1
  35.3 4.2 %broadcast_multiply_fusion = bf16[64,64,4,64]{3,2,1,0:T(4,128)(2,1)} fusion(bf16[64,64,64]{2,1,0:T(8,128)(2,1)S(1)} %copy-done.1, bf16[64,4]{1,0:T(8,128)(2,1)S(1)} %copy.12), kind=kLoop, calls=%fused_computation.9 | loop fusion | flops 1048576 | bytes 2621952 | tf_op jit(solution)/shard_map/mul | solution.py:49
  39.5 7.0 %mul.38 = bf16[4096,256]{1,0:T(8,128)(2,1)} reshape(bf16[64,64,4,64]{3,2,1,0:T(4,128)(2,1)} %broadcast_multiply_fusion) | data formatting | bytes 4194304 | tf_op jit(solution)/shard_map/mul | solution.py:49
  46.5 0.0 collective-permute-done
  46.5 0.0 copy-start.2
  46.5 1.0 copy-done.2
  47.5 0.0 collective-permute-done.1
  47.5 2.2 pad_maximum_fusion
  49.7 18.2 %gather_fusion = bf16[768,64,64]{2,1,0:T(8,128)(2,1)} fusion(bf16[192,64,64]{2,1,0:T(8,128)(2,1)S(1)} %pad_maximum_fusion, s32[1024]{0:T(1024)S(1)} %pad_clamp_fusion), kind=kCustom, calls=%fused_computation | custom fusion | bytes 12585984 | tf_op jit(solution)/shard_map/jit(_take)/gather | solution.py:30
  67.8 16.6 %copy.15 = bf16[64,12,64,64]{2,3,1,0:T(8,128)(2,1)} copy(bf16[64,12,64,64]{3,2,1,0:T(8,128)(2,1)} %bitcast.19) | data formatting | bytes 12582912 | tf_op jit(solution)/shard_map/jit(_take)/gather | solution.py:30
  84.5 21.7 %fusion.4 = f32[64,64,12,64]{1,3,2,0:T(8,128)} fusion(bf16[64,64,12,64]{3,2,1,0:T(8,128)(2,1)} %reshape.77, bf16[64,12,64,64]{2,3,1,0:T(8,128)(2,1)} %copy.15, pred[64,12]{1,0:T(8,128)(4,1)S(1)} %copy.13), kind=kOutput, calls=%fused_computation.6 | convolution fusion | flops 405798912 | bytes 25166592 | tf_op jit(solution)/shard_map/ixky,ikyz->ixkz/dot_general | solution.py:32
  106.2 31.1 %copy.18 = f32[64,64,12,64]{3,2,1,0:T(8,128)} copy(f32[64,64,12,64]{1,3,2,0:T(8,128)} %fusion.4) | data formatting | bytes 25165824 | tf_op jit(solution)/shard_map/ixky,ikyz->ixkz/transpose | solution.py:32
  137.3 25.0 %convert_bitcast_fusion = bf16[64,64,12,64]{3,2,1,0:T(8,128)(2,1)} fusion(f32[64,64,12,64]{3,2,1,0:T(8,128)} %copy.18, s32[64,12]{1,0:T(8,128)S(1)} %copy.17, pred[64]{0:T(512)(128)(4,1)S(1)} %iota_compare_fusion.2), kind=kOutput, calls=%fused_computation.1 | convolution fusion | flops 456148992 | bytes 18877504 | tf_op jit(solution)/shard_map/ikt,ixkz->ixtz/dot_general | solution.py:40
  162.3 0.0 copy-start
  162.3 20.9 %reshape.98 = bf16[4096,768]{1,0:T(8,128)(2,1)} reshape(bf16[64,64,12,64]{3,2,1,0:T(8,128)(2,1)} %convert_bitcast_fusion) | data formatting | bytes 12582912 | tf_op jit(solution)/shard_map/reshape | solution.py:43
  183.1 0.0 copy-done
  183.2 4.6 %convolution_convert_fusion = bf16[256,768]{1,0:T(8,128)(2,1)S(1)} fusion(bf16[4096,256]{1,0:T(8,128)(2,1)S(1)} %copy-done, bf16[4096,768]{1,0:T(8,128)(2,1)} %reshape.98), kind=kOutput, calls=%fused_computation.10 | convolution fusion | flops 1610809344 | bytes 8781824 | tf_op jit(solution)/shard_map/dot_general | solution.py:51
  187.8 0.7 collective-permute-start.2
  188.5 0.0 collective-permute-done.2
  188.5 0.0 copy-start.3
  188.5 0.7 copy-done.3
  189.2 0.0 all-gather.3.cloned.1.call-update
  189.2 94.7 %all-gather.3.cloned.1.call-done = bf16[2048,768]{1,0:T(8,128)(2,1)} async-done(((bf16[256,768]{1,0:T(8,128)(2,1)}), bf16[2048,768]{1,0:T(8,128)(2,1)}) %all-gather.3.cloned.1.call-update) | async-done | bytes 3145744 | tf_op jit(solution)/shard_map/all_gather | solution.py:63
  283.9 5.4 %convert.1 = f32[32,64,768]{2,1,0:T(8,128)} convert(bf16[32,64,768]{2,1,0:T(8,128)(2,1)} %bitcast.20) | non-fusion elementwise | flops 1572864 | bytes 9437184 | tf_op jit(solution)/shard_map/reshape | solution.py:65
  (3 shorter events, 0.0 us)
Async XLA Ops:
  6.5 28.8 %copy-start.1 = (bf16[64,64,64]{2,1,0:T(8,128)(2,1)S(1)}, bf16[64,64,64]{2,1,0:T(8,128)(2,1)}, u32[]{:S(2)}) copy-start(bf16[64,64,64]{2,1,0:T(8,128)(2,1)} %param.6) | copy-start | bytes 1572868
  6.5 277.4 %all-gather.3.cloned.1.call-start = ((), (), s32[]{:S(2)}) async-start(), calls=%async_computation | async-start | bytes 3538944 | tf_op jit(solution)/shard_map/all_gather | solution.py:63
  6.5 39.9 %collective-permute-start = (bf16[64,64,64]{2,1,0:T(8,128)(2,1)}, bf16[64,64,64]{2,1,0:T(8,128)(2,1)S(1)}, u32[]{:S(2)}, u32[]{:S(2)}) collective-permute-start(bf16[64,64,64]{2,1,0:T(8,128)(2,1)} %param.6), channel_id=1, source_target_pairs={{0,1},{1,2},{2,3},{3,4},{4,5},{5,6},{6,7},{7,8},{8,9},{9,10},{10,1... | collective-permute-start | bytes 1572872 | tf_op jit(solution)/shard_map/ppermute | solution.py:14
  8.6 38.9 %collective-permute-start.1 = (bf16[64,64,64]{2,1,0:T(8,128)(2,1)}, bf16[64,64,64]{2,1,0:T(8,128)(2,1)}, u32[]{:S(2)}, u32[]{:S(2)}) collective-permute-start(bf16[64,64,64]{2,1,0:T(8,128)(2,1)} %param.6), channel_id=1, source_target_pairs={{1,0},{2,1},{3,2},{4,3},{5,4},{6,5},{7,6},{8,7},{9,8},{10,9},{11,1... | collective-permute-start | bytes 1572872 | tf_op jit(solution)/shard_map/ppermute | solution.py:17
  46.5 1.0 copy-start.2
  162.3 20.9 %copy-start = (bf16[4096,256]{1,0:T(8,128)(2,1)S(1)}, bf16[4096,256]{1,0:T(8,128)(2,1)}, u32[]{:S(2)}) copy-start(bf16[4096,256]{1,0:T(8,128)(2,1)} %mul.38) | copy-start | bytes 6291460
  187.8 0.7 collective-permute-start.2
  188.5 0.7 copy-start.3
Sparse Core Ops, SparseCore 0:
  189.4 94.5 all-gather.2

commit v2 on v1

v2 whole, which is shorter than its diff:
```python
import jax
import jax.numpy as jnp
from jax import lax
from jax.experimental import pallas as pl
from jax.experimental.pallas import tpu as pltpu
from jax.sharding import PartitionSpec as P

AGG_DEV = 4


def coarse_kernel(cols_ref, slots_ref, aggs_ref, live_ref, f_ref, wl_ref, wr_ref, pt_ref, o_ref, even_ref, odd_ref):
    step = pl.program_id(0)
    rows = f_ref.shape[0]
    width = pt_ref.shape[1]
    pairs = f_ref.shape[2] // (2 * width)
    slots = even_ref.shape[0]

    @pl.when(step == 0)
    def _():
        o_ref[...] = jnp.zeros_like(o_ref)

    lane = lax.broadcasted_iota(jnp.int32, (width, 2 * width), 1)
    low_half = lane < width

    def row(r, carry):
        i = step * rows + r
        even_ref[...] = jnp.zeros_like(even_ref)
        odd_ref[...] = jnp.zeros_like(odd_ref)
        for j in range(pairs):
            first = i * (2 * pairs) + 2 * j
            block = jnp.concatenate([wl_ref[cols_ref[first]], wr_ref[cols_ref[first + 1]]], axis=0)
            part = jnp.dot(
                f_ref[r, :, 2 * width * j : 2 * width * (j + 1)], block, preferred_element_type=jnp.float32
            )
            t_even = slots_ref[first]
            t_odd = slots_ref[first + 1]
            even_ref[t_even] += part
            odd_ref[t_odd] += part
        live = i < live_ref[0]
        tiles = []
        for u in range(slots // 2):
            left = even_ref[2 * u] + pltpu.roll(odd_ref[2 * u], width, 1)
            right = pltpu.roll(even_ref[2 * u + 1], width, 1) + odd_ref[2 * u + 1]
            tiles.append(jnp.where(low_half, left, right))
        sums = jnp.concatenate(tiles, axis=1)
        sums = jnp.where(live, sums, 0.0).astype(jnp.bfloat16).astype(pt_ref.dtype)
        a = aggs_ref[i]
        o_ref[a] += jnp.dot(pt_ref[r], sums, preferred_element_type=jnp.float32)
        return carry

    lax.fori_loop(0, rows, row, 0)


def coarse_rows(fine, ghosts, local_rows, slots, aggs, live_count, rows=8, interpret=False):
    capacity, width, span = fine.shape
    slot_width = 3 * AGG_DEV
    ghost_count = ghosts.shape[0]
    wl = jnp.pad(ghosts, ((0, 0), (0, 0), (0, width)))
    wr = jnp.pad(ghosts, ((0, 0), (0, 0), (width, 0)))
    transposed = jnp.swapaxes(ghosts[capacity : 2 * capacity], 1, 2)
    grid_spec = pltpu.PrefetchScalarGridSpec(
        num_scalar_prefetch=4,
        grid=(capacity // rows,),
        in_specs=[
            pl.BlockSpec((rows, width, span), lambda b, *_: (b, 0, 0)),
            pl.BlockSpec((ghost_count, width, 2 * width), lambda b, *_: (0, 0, 0)),
            pl.BlockSpec((ghost_count, width, 2 * width), lambda b, *_: (0, 0, 0)),
            pl.BlockSpec((rows, width, width), lambda b, *_: (b, 0, 0)),
        ],
        out_specs=pl.BlockSpec((AGG_DEV, width, slot_width * width), lambda b, *_: (0, 0, 0)),
        scratch_shapes=[
            pltpu.VMEM((slot_width, width, 2 * width), jnp.float32),
            pltpu.VMEM((slot_width, width, 2 * width), jnp.float32),
        ],
    )
    return pl.pallas_call(
        coarse_kernel,
        grid_spec=grid_spec,
        out_shape=jax.ShapeDtypeStruct((AGG_DEV, width, slot_width * width), jnp.float32),
        compiler_params=pltpu.CompilerParams(dimension_semantics=("arbitrary",)),
        interpret=interpret,
    )(local_rows.reshape(-1), slots.reshape(-1), aggs, live_count, fine, wl, wr, transposed)


def extended(block, sides, width):
    for axis, dim in sides:
        count = lax.axis_size(axis)
        forward = [(i, i + 1) for i in range(count - 1)]
        backward = [(target, source) for source, target in forward]
        low = lax.ppermute(
            lax.slice_in_dim(block, block.shape[dim] - width, None, axis=dim), axis, forward
        )
        high = lax.ppermute(lax.slice_in_dim(block, 0, width, axis=dim), axis, backward)
        block = jnp.concatenate([low, block, high], axis=dim)
    return block


def local(fine_matrix_blocks, prolongator, block_columns, block_aggregates, live_counts):
    capacity = fine_matrix_blocks.shape[0]
    position = lax.axis_index(("grp", "dom"))
    ghosts = extended(prolongator, ((("grp", "dom"), 0),), capacity)
    local_rows = jnp.clip(block_columns - (position - 1) * capacity, 0, 3 * capacity - 1)
    slots = jnp.clip(AGG_DEV * (local_rows // capacity) + block_aggregates % AGG_DEV, 0, 3 * AGG_DEV - 1)
    aggs = block_aggregates[:, 0] % AGG_DEV
    coarse = coarse_rows(fine_matrix_blocks, ghosts, local_rows, slots, aggs, live_counts)
    groups_count = lax.axis_size("grp")
    places = lax.axis_size("dom")
    step_stride = places // groups_count
    pairs = [
        (g * places + q, g * places + (q + step_stride * g) % places)
        for g in range(groups_count)
        for q in range(places)
    ]
    rotated = lax.ppermute(coarse.astype(jnp.bfloat16), ("grp", "dom"), pairs)
    copies = jnp.broadcast_to(rotated[None], (groups_count,) + rotated.shape)
    result = lax.all_to_all(copies, "grp", 0, 0, tiled=True).astype(jnp.float32)
    return result.reshape((groups_count * AGG_DEV,) + coarse.shape[1:])


def solution(mesh):
    return jax.shard_map(
        local,
        mesh=mesh,
        in_specs=(
            P(("grp", "dom"), None, None),
            P(("grp", "dom"), None, None),
            P(("grp", "dom"), None),
            P(("grp", "dom"), None),
            P(("grp", "dom")),
        ),
        out_specs=P("dom", None, None),
        check_vma=False,
    )
```

time: 300 us -> 141 us (0.47)
  the two profiles are of different devices: /device:TPU:96 before, /device:TPU:160 now
where the time goes in v2:
time: 141 us; the launch traced here: 140 us
  blocking collectives  72.9 us (52%)
  Pallas kernels  38.4 us (27%)
  local copies, waits for them, and re-layouts  9.17 us (7%)
  other arithmetic  6.83 us (5%)
  starting transfers between devices  6.37 us (5%)
  waiting for transfers between devices  5.91 us (4%)
    all_to_all x1, blocking collectives, local(): result = lax.all_to_all(copies, 'grp', 0, 0, tiled=True).astype(jnp.float32)  72.9 us
    pallas_call x1, Pallas kernels, coarse_rows(): pl.pallas_call(coarse_kernel, grid_spec=grid_spec, out_shape=jax.ShapeDty...  38.4 us
    pad x1, local copies, waits for them, and re-layouts, coarse_rows(): wr = jnp.pad(ghosts, ((0, 0), (0, 0), (width, 0)))  4.63 us
    ppermute x1, waiting for transfers between devices, extended(): lax.ppermute(lax.slice_in_dim(block, block.shape[dim] - width, None, axis...  4.28 us
    reshape x1, other arithmetic, local(): return result.reshape((groups_count * AGG_DEV,) + coarse.shape[1:])  3.7 us
    ppermute x1, starting transfers between devices, extended(): lax.ppermute(lax.slice_in_dim(block, 0, width, axis=dim), axis, backward)  3.64 us
  transfers between devices with their start and end apart: 3, of which 2 were waited for; matrix products, arithmetic and copies ran while one was open for 4% of the time, Pallas kernels for 0%

profile of v2, /device:TPU:160, one launch (start us, length us, event | category | flops | bytes accessed | tf_op | source)
XLA Modules:
  0.0 140.3 jit_solution(7893548553838885133)
XLA Ops:
  0.0 0.0 copy-start
  0.0 2.0 %collective-permute-start = (bf16[64,64,64]{2,1,0:T(8,128)(2,1)}, bf16[64,64,64]{2,1,0:T(8,128)(2,1)S(1)}, u32[]{:S(2)}, u32[]{:S(2)}) collective-permute-start(bf16[64,64,64]{2,1,0:T(8,128)(2,1)} %param.6), channel_id=1, source_target_pairs={{0,1},{1,2},{2,3},{3,4},{4,5},{5,6},{6,7},{7,8},{8,9},{9,10},{10,1... | collective-permute-start | bytes 1572872 | tf_op jit(solution)/shard_map/ppermute | solution.py:90
  2.1 3.6 %collective-permute-start.1 = (bf16[64,64,64]{2,1,0:T(8,128)(2,1)}, bf16[64,64,64]{2,1,0:T(8,128)(2,1)S(1)}, u32[]{:S(2)}, u32[]{:S(2)}) collective-permute-start(bf16[64,64,64]{2,1,0:T(8,128)(2,1)} %param.6), channel_id=1, source_target_pairs={{1,0},{2,1},{3,2},{4,3},{5,4},{6,5},{7,6},{8,7},{9,8},{10,9},{11,1... | collective-permute-start | bytes 1572872 | tf_op jit(solution)/shard_map/ppermute | solution.py:93
  5.7 0.7 fusion.3
  6.4 2.3 %copy.9 = bf16[64,64,64]{1,2,0:T(8,128)(2,1)} copy(bf16[64,64,64]{2,1,0:T(8,128)(2,1)} %param.6) | data formatting | bytes 1048576 | tf_op args[1]
  8.7 0.1 copy.7
  8.8 0.7 reshape.13.cols_ref
  9.5 0.1 copy.8
  9.6 0.7 reshape.14.slots_ref
  10.9 1.2 and_select_fusion.aggs_ref
  12.2 4.3 %collective-permute-done = bf16[64,64,64]{2,1,0:T(8,128)(2,1)S(1)} collective-permute-done((bf16[64,64,64]{2,1,0:T(8,128)(2,1)}, bf16[64,64,64]{2,1,0:T(8,128)(2,1)S(1)}, u32[]{:S(2)}, u32[]{:S(2)}) %collective-permute-start) | collective-permute-done | bytes 524320 | tf_op jit(solution)/shard_map/ppermute | solution.py:90
  16.5 0.1 constant_dynamic-update-slice_fusion.2
  16.5 0.0 copy-done
  16.5 0.1 constant_dynamic-update-slice_fusion.1
  16.7 1.6 %collective-permute-done.1 = bf16[64,64,64]{2,1,0:T(8,128)(2,1)S(1)} collective-permute-done((bf16[64,64,64]{2,1,0:T(8,128)(2,1)}, bf16[64,64,64]{2,1,0:T(8,128)(2,1)S(1)}, u32[]{:S(2)}, u32[]{:S(2)}) %collective-permute-start.1) | collective-permute-done | bytes 524320 | tf_op jit(solution)/shard_map/ppermute | solution.py:93
  18.3 0.1 constant_dynamic-update-slice_fusion
  18.5 4.6 %fusion.7 = (bf16[192,64,128]{2,1,0:T(8,128)(2,1)}, bf16[192,64,128]{2,1,0:T(8,128)(2,1)}) fusion(bf16[192,64,64]{2,1,0:T(8,128)(2,1)S(1)} %constant_dynamic-update-slice_fusion), kind=kLoop, calls=%fused_computation.23 | loop fusion | bytes 7864320 | tf_op jit(solution)/shard_map/jit(_pad)/pad | solution.py:59
  23.1 38.4 %shard_map.55 = f32[4,64,768]{2,1,0:T(8,128)} custom-call(s32[768]{0:T(1024)} %reshape.13.cols_ref, s32[768]{0:T(1024)} %reshape.14.slots_ref, s32[64]{0:T(128)} %and_select_fusion.aggs_ref, s32[1]{0:T(128)S(6)} %copy.12.live_ref, bf16[64,64,768]{2,1,0:T(8,128)(2,1)} %f_ref.1, bf16[192,64,128]{2,1,0:T(8,128)(2,1)} %get-tuple-element.8.wl_ref, ...), custom_call_target="tpu_custom_call" | custom-call | tf_op jit(solution)/shard_map/pallas_call | solution.py:76
  61.5 1.2 convert_element_type.8
  62.6 0.7 collective-permute-start.2
  63.3 0.0 collective-permute-done.2
  63.4 0.4 broadcast_in_dim.2
  63.7 72.9 %all_to_all.5 = bf16[8,4,64,768]{3,2,1,0:T(8,128)(2,1)S(1)} all-to-all(bf16[8,4,64,768]{3,2,1,0:T(8,128)(2,1)S(1)} %broadcast_in_dim.2), channel_id=1, replica_groups=mesh['grp'=8,'dom'=32] {'grp'}, dimensions={0} | all-to-all | bytes 6291456 | tf_op jit(solution)/shard_map/all_to_all | solution.py:116
  136.6 3.7 %bitcast_convert_fusion = f32[32,64,768]{2,1,0:T(8,128)} fusion(bf16[8,4,64,768]{3,2,1,0:T(8,128)(2,1)S(1)} %all_to_all.5), kind=kLoop, calls=%fused_computation | loop fusion | flops 1572864 | bytes 9437184 | tf_op jit(solution)/shard_map/reshape | solution.py:117
Async XLA Ops:
  0.0 16.5 %copy-start = (bf16[64,64,64]{2,1,0:T(8,128)(2,1)S(1)}, bf16[64,64,64]{2,1,0:T(8,128)(2,1)}, u32[]{:S(2)}) copy-start(bf16[64,64,64]{2,1,0:T(8,128)(2,1)} %param.6) | copy-start | bytes 1572868
  0.0 16.4 %collective-permute-start = (bf16[64,64,64]{2,1,0:T(8,128)(2,1)}, bf16[64,64,64]{2,1,0:T(8,128)(2,1)S(1)}, u32[]{:S(2)}, u32[]{:S(2)}) collective-permute-start(bf16[64,64,64]{2,1,0:T(8,128)(2,1)} %param.6), channel_id=1, source_target_pairs={{0,1},{1,2},{2,3},{3,4},{4,5},{5,6},{6,7},{7,8},{8,9},{9,10},{10,1... | collective-permute-start | bytes 1572872 | tf_op jit(solution)/shard_map/ppermute | solution.py:90
  2.1 16.3 %collective-permute-start.1 = (bf16[64,64,64]{2,1,0:T(8,128)(2,1)}, bf16[64,64,64]{2,1,0:T(8,128)(2,1)S(1)}, u32[]{:S(2)}, u32[]{:S(2)}) collective-permute-start(bf16[64,64,64]{2,1,0:T(8,128)(2,1)} %param.6), channel_id=1, source_target_pairs={{1,0},{2,1},{3,2},{4,3},{5,4},{6,5},{7,6},{8,7},{9,8},{10,9},{11,1... | collective-permute-start | bytes 1572872 | tf_op jit(solution)/shard_map/ppermute | solution.py:93
  62.6 0.7 collective-permute-start.2

commit v3 on v2

v3 whole, which is shorter than its diff:
```python
import functools
import jax
import jax.numpy as jnp
from jax import lax
from jax.experimental import pallas as pl
from jax.experimental.pallas import tpu as pltpu
from jax.sharding import PartitionSpec as P

AGG_DEV = 4


def coarse_kernel(cols_ref, aggs_ref, live_ref, base_ref, f_ref, g_ref, p_ref, o_ref, even_ref, odd_ref, *, group, transpose_lhs, capacity):
    step = pl.program_id(0)
    rows = f_ref.shape[0]
    width = p_ref.shape[1]
    blocks = f_ref.shape[2] // width
    slots = even_ref.shape[0]
    ghost_count = g_ref.shape[0]

    @pl.when(step == 0)
    def _():
        o_ref[...] = jnp.zeros_like(o_ref)

    lane = lax.broadcasted_iota(jnp.int32, (width, 2 * width), 1)
    low_half = lane < width
    base = base_ref[0]

    def place(r_i, k):
        c = jnp.clip(cols_ref[r_i, k] - base, 0, ghost_count - 1)
        t = AGG_DEV * (c // capacity) + jnp.bitwise_and(aggs_ref[r_i, k], AGG_DEV - 1)
        return c, t

    def row(r, carry):
        i = step * rows + r
        even_ref[...] = jnp.zeros_like(even_ref)
        odd_ref[...] = jnp.zeros_like(odd_ref)
        for j in range(blocks // group):
            ks = [group * j + m for m in range(group)]
            placed = [place(i, k) for k in ks]
            pieces = []
            for m, (c, _) in enumerate(placed):
                tile = g_ref[c]
                pieces.append(jnp.where(low_half if m % 2 == 0 else ~low_half, tile, jnp.zeros_like(tile)))
            if group == 2:
                block = jnp.concatenate(pieces, axis=0)
            else:
                zero = jnp.zeros((2 * width, 2 * width), pieces[0].dtype)
                top = jnp.concatenate([jnp.concatenate(pieces[:2], axis=0), zero], axis=1)
                bottom = jnp.concatenate([zero, jnp.concatenate(pieces[2:], axis=0)], axis=1)
                block = jnp.concatenate([top, bottom], axis=0)
            part = jnp.dot(
                f_ref[r, :, group * width * j : group * width * (j + 1)], block, preferred_element_type=jnp.float32
            )
            for h in range(group // 2):
                half = part[:, 2 * width * h : 2 * width * (h + 1)]
                even_ref[placed[2 * h][1]] += half
                odd_ref[placed[2 * h + 1][1]] += half
        live = i < live_ref[0]
        tiles = []
        for u in range(slots // 2):
            left = even_ref[2 * u] + pltpu.roll(odd_ref[2 * u], width, 1)
            right = pltpu.roll(even_ref[2 * u + 1], width, 1) + odd_ref[2 * u + 1]
            tiles.append(jnp.where(low_half, left, right))
        sums = jnp.concatenate(tiles, axis=1)
        sums = jnp.where(live, sums, 0.0).astype(jnp.bfloat16).astype(p_ref.dtype)
        a = jnp.bitwise_and(aggs_ref[i, 0], AGG_DEV - 1)
        if transpose_lhs:
            contrib = lax.dot_general(p_ref[r], sums, (((0,), (0,)), ((), ())), preferred_element_type=jnp.float32)
        else:
            contrib = jnp.dot(p_ref[r].T, sums, preferred_element_type=jnp.float32)
        o_ref[a] += contrib
        return carry

    lax.fori_loop(0, rows, row, 0)


def coarse_rows(fine, ghosts, own, cols, aggs, live_count, base, rows=8, group=2, transpose_lhs=True, interpret=False):
    capacity, width, span = fine.shape
    slot_width = 3 * AGG_DEV
    ghost_count = ghosts.shape[0]
    doubled = jnp.concatenate([ghosts, ghosts], axis=2)
    grid_spec = pltpu.PrefetchScalarGridSpec(
        num_scalar_prefetch=4,
        grid=(capacity // rows,),
        in_specs=[
            pl.BlockSpec((rows, width, span), lambda b, *_: (b, 0, 0)),
            pl.BlockSpec((ghost_count, width, 2 * width), lambda b, *_: (0, 0, 0)),
            pl.BlockSpec((rows, width, width), lambda b, *_: (b, 0, 0)),
        ],
        out_specs=pl.BlockSpec((AGG_DEV, width, slot_width * width), lambda b, *_: (0, 0, 0)),
        scratch_shapes=[
            pltpu.VMEM((slot_width, width, 2 * width), jnp.float32),
            pltpu.VMEM((slot_width, width, 2 * width), jnp.float32),
        ],
    )
    kernel = functools.partial(coarse_kernel, group=group, transpose_lhs=transpose_lhs, capacity=capacity)
    return pl.pallas_call(
        kernel,
        grid_spec=grid_spec,
        out_shape=jax.ShapeDtypeStruct((AGG_DEV, width, slot_width * width), jnp.float32),
        compiler_params=pltpu.CompilerParams(dimension_semantics=("arbitrary",)),
        interpret=interpret,
    )(cols, aggs, live_count, base, fine, doubled, own)


def extended(block, sides, width):
    for axis, dim in sides:
        count = lax.axis_size(axis)
        forward = [(i, i + 1) for i in range(count - 1)]
        backward = [(target, source) for source, target in forward]
        low = lax.ppermute(
            lax.slice_in_dim(block, block.shape[dim] - width, None, axis=dim), axis, forward
        )
        high = lax.ppermute(lax.slice_in_dim(block, 0, width, axis=dim), axis, backward)
        block = jnp.concatenate([low, block, high], axis=dim)
    return block


def local(fine_matrix_blocks, prolongator, block_columns, block_aggregates, live_counts):
    capacity = fine_matrix_blocks.shape[0]
    position = lax.axis_index(("grp", "dom"))
    ghosts = extended(prolongator, ((("grp", "dom"), 0),), capacity)
    base = jnp.reshape((position - 1) * capacity, (1,)).astype(jnp.int32)
    coarse = coarse_rows(
        fine_matrix_blocks, ghosts, prolongator, block_columns, block_aggregates, live_counts, base
    )
    groups_count = lax.axis_size("grp")
    places = lax.axis_size("dom")
    step_stride = places // groups_count
    pairs = [
        (g * places + q, g * places + (q + step_stride * g) % places)
        for g in range(groups_count)
        for q in range(places)
    ]
    rotated = lax.ppermute(coarse.astype(jnp.bfloat16), ("grp", "dom"), pairs)
    copies = jnp.broadcast_to(rotated[None], (groups_count,) + rotated.shape)
    result = lax.all_to_all(copies, "grp", 0, 0, tiled=True).astype(jnp.float32)
    return result.reshape((groups_count * AGG_DEV,) + coarse.shape[1:])


def solution(mesh):
    return jax.shard_map(
        local,
        mesh=mesh,
        in_specs=(
            P(("grp", "dom"), None, None),
            P(("grp", "dom"), None, None),
            P(("grp", "dom"), None),
            P(("grp", "dom"), None),
            P(("grp", "dom")),
        ),
        out_specs=P("dom", None, None),
        check_vma=False,
    )
```

time: 141 us -> 141 us (level)
  the two profiles are of different devices: /device:TPU:160 before, /device:TPU:96 now
where the time goes in v3:
time: 141 us; the launch traced here: 140 us
  blocking collectives  71.5 us (51%)
  Pallas kernels  40.1 us (28%)
  waiting for transfers between devices  10.5 us (7%)
  other arithmetic  9.56 us (7%)
  starting transfers between devices  5 us (4%)
  local copies, waits for them, and re-layouts  3.14 us (2%)
    all_to_all x1, blocking collectives, local(): result = lax.all_to_all(copies, 'grp', 0, 0, tiled=True).astype(jnp.float32)  71.5 us
    pallas_call x1, Pallas kernels, coarse_rows(): pl.pallas_call(kernel, grid_spec=grid_spec, out_shape=jax.ShapeDtypeStruc...  40.1 us
    ppermute x1, waiting for transfers between devices, extended(): lax.ppermute(lax.slice_in_dim(block, 0, width, axis=dim), axis, backward)  6.75 us
    concatenate x1, other arithmetic, coarse_rows(): doubled = jnp.concatenate([ghosts, ghosts], axis=2)  4.69 us
    ppermute x1, waiting for transfers between devices, extended(): lax.ppermute(lax.slice_in_dim(block, block.shape[dim] - width, None, axis...  3.72 us
    reshape x1, other arithmetic, local(): return result.reshape((groups_count * AGG_DEV,) + coarse.shape[1:])  3.7 us
  transfers between devices with their start and end apart: 3, of which 2 were waited for; matrix products, arithmetic and copies ran while one was open for 2% of the time, Pallas kernels for 0%

profile of v3, /device:TPU:96, one launch (start us, length us, event | category | flops | bytes accessed | tf_op | source)
XLA Modules:
  0.0 140.5 jit_solution(12152608970085395457)
XLA Ops:
  0.0 1.9 %collective-permute-start.1 = (bf16[64,64,64]{2,1,0:T(8,128)(2,1)}, bf16[64,64,64]{2,1,0:T(8,128)(2,1)S(1)}, u32[]{:S(2)}, u32[]{:S(2)}) collective-permute-start(bf16[64,64,64]{2,1,0:T(8,128)(2,1)} %p_ref.1), channel_id=1, source_target_pairs={{1,0},{2,1},{3,2},{4,3},{5,4},{6,5},{7,6},{8,7},{9,8},{10,9},{11,1... | collective-permute-start | bytes 1572872 | tf_op jit(solution)/shard_map/ppermute | solution.py:114
  1.9 2.4 %collective-permute-start = (bf16[64,64,64]{2,1,0:T(8,128)(2,1)}, bf16[64,64,64]{2,1,0:T(8,128)(2,1)S(1)}, u32[]{:S(2)}, u32[]{:S(2)}) collective-permute-start(bf16[64,64,64]{2,1,0:T(8,128)(2,1)} %p_ref.1), channel_id=1, source_target_pairs={{0,1},{1,2},{2,3},{3,4},{4,5},{5,6},{6,7},{7,8},{8,9},{9,10},{10,1... | collective-permute-start | bytes 1572872 | tf_op jit(solution)/shard_map/ppermute | solution.py:111
  5.0 1.4 copy.6.cols_ref
  6.4 1.4 copy.7.aggs_ref
  7.8 6.8 %collective-permute-done.1 = bf16[64,64,64]{2,1,0:T(8,128)(2,1)S(1)} collective-permute-done((bf16[64,64,64]{2,1,0:T(8,128)(2,1)}, bf16[64,64,64]{2,1,0:T(8,128)(2,1)S(1)}, u32[]{:S(2)}, u32[]{:S(2)}) %collective-permute-start.1) | collective-permute-done | bytes 524320 | tf_op jit(solution)/shard_map/ppermute | solution.py:114
  14.5 3.7 %collective-permute-done = bf16[64,64,64]{2,1,0:T(8,128)(2,1)S(1)} collective-permute-done((bf16[64,64,64]{2,1,0:T(8,128)(2,1)}, bf16[64,64,64]{2,1,0:T(8,128)(2,1)S(1)}, u32[]{:S(2)}, u32[]{:S(2)}) %collective-permute-start) | collective-permute-done | bytes 524320 | tf_op jit(solution)/shard_map/ppermute | solution.py:111
  18.2 4.7 %maximum_maximum_fusion.g_ref = bf16[192,64,128]{2,1,0:T(8,128)(2,1)} fusion(bf16[64,64,64]{2,1,0:T(8,128)(2,1)S(1)} %collective-permute-done.1, bf16[64,64,64]{2,1,0:T(8,128)(2,1)} %p_ref.1, bf16[64,64,64]{2,1,0:T(8,128)(2,1)S(1)} %collective-permute-done), kind=kLoop, calls=%fused_computation | loop fusion | flops 18874368 | bytes 4718592 | tf_op jit(solution)/shard_map/concatenate | solution.py:81
  22.9 40.1 %shard_map.55 = f32[4,64,768]{2,1,0:T(8,128)} custom-call(s32[64,12]{1,0:T(8,128)} %copy.6.cols_ref, s32[64,12]{1,0:T(8,128)} %copy.7.aggs_ref, s32[1]{0:T(128)S(6)} %copy.8.live_ref, s32[1]{0:T(128)} %bitcast.base_ref, bf16[64,64,768]{2,1,0:T(8,128)(2,1)} %f_ref.1, bf16[192,64,128]{2,1,0:T(8,128)(2,1)} %maximum_maximum_fusion.g_ref, bf16[64,64,64]{2,1,0:T(8,128)(2,1)} %p_ref.1), custom_call_target="tpu_custom_call" | custom-call | tf_op jit(solution)/shard_map/pallas_call | solution.py:97
  63.1 1.2 convert_element_type.4
  64.2 0.7 collective-permute-start.2
  64.9 0.0 collective-permute-done.2
  64.9 0.4 broadcast_in_dim.2
  65.3 71.5 %all_to_all.5 = bf16[8,4,64,768]{3,2,1,0:T(8,128)(2,1)S(1)} all-to-all(bf16[8,4,64,768]{3,2,1,0:T(8,128)(2,1)S(1)} %broadcast_in_dim.2), channel_id=1, replica_groups=mesh['grp'=8,'dom'=32] {'grp'}, dimensions={0} | all-to-all | bytes 6291456 | tf_op jit(solution)/shard_map/all_to_all | solution.py:137
  136.8 3.7 %bitcast_convert_fusion = f32[32,64,768]{2,1,0:T(8,128)} fusion(bf16[8,4,64,768]{3,2,1,0:T(8,128)(2,1)S(1)} %all_to_all.5), kind=kLoop, calls=%fused_computation.1 | loop fusion | flops 1572864 | bytes 9437184 | tf_op jit(solution)/shard_map/reshape | solution.py:138
Async XLA Ops:
  0.0 14.5 %collective-permute-start.1 = (bf16[64,64,64]{2,1,0:T(8,128)(2,1)}, bf16[64,64,64]{2,1,0:T(8,128)(2,1)S(1)}, u32[]{:S(2)}, u32[]{:S(2)}) collective-permute-start(bf16[64,64,64]{2,1,0:T(8,128)(2,1)} %p_ref.1), channel_id=1, source_target_pairs={{1,0},{2,1},{3,2},{4,3},{5,4},{6,5},{7,6},{8,7},{9,8},{10,9},{11,1... | collective-permute-start | bytes 1572872 | tf_op jit(solution)/shard_map/ppermute | solution.py:114
  1.9 16.3 %collective-permute-start = (bf16[64,64,64]{2,1,0:T(8,128)(2,1)}, bf16[64,64,64]{2,1,0:T(8,128)(2,1)S(1)}, u32[]{:S(2)}, u32[]{:S(2)}) collective-permute-start(bf16[64,64,64]{2,1,0:T(8,128)(2,1)} %p_ref.1), channel_id=1, source_target_pairs={{0,1},{1,2},{2,3},{3,4},{4,5},{5,6},{6,7},{7,8},{8,9},{9,10},{10,1... | collective-permute-start | bytes 1572872 | tf_op jit(solution)/shard_map/ppermute | solution.py:111
  64.2 0.7 collective-permute-start.2

commit v4 on v3

--- a/solution.py
+++ b/solution.py
@@ -9,7 +9,9 @@
 AGG_DEV = 4
 
 
-def coarse_kernel(cols_ref, aggs_ref, live_ref, base_ref, f_ref, g_ref, p_ref, o_ref, even_ref, odd_ref, *, group, transpose_lhs, capacity):
+def coarse_kernel(
+    cols_ref, aggs_ref, live_ref, base_ref, f_ref, g_ref, p_ref, o_ref, even_ref, odd_ref, *, group, transpose_lhs, capacity, half
+):
     step = pl.program_id(0)
     rows = f_ref.shape[0]
     width = p_ref.shape[1]
@@ -32,6 +34,16 @@
 
     def row(r, carry):
         i = step * rows + r
+        a = jnp.bitwise_and(aggs_ref[i, 0], AGG_DEV - 1)
+        kept = o_ref.shape[0]
+
+        @pl.when(a // kept == half)
+        def _():
+            one_row(r, i, a - kept * half)
+
+        return carry
+
+    def one_row(r, i, a):
         even_ref[...] = jnp.zeros_like(even_ref)
         odd_ref[...] = jnp.zeros_like(odd_ref)
         for j in range(blocks // group):
@@ -52,9 +64,9 @@
                 f_ref[r, :, group * width * j : group * width * (j + 1)], block, preferred_element_type=jnp.float32
             )
             for h in range(group // 2):
-                half = part[:, 2 * width * h : 2 * width * (h + 1)]
-                even_ref[placed[2 * h][1]] += half
-                odd_ref[placed[2 * h + 1][1]] += half
+                piece = part[:, 2 * width * h : 2 * width * (h + 1)]
+                even_ref[placed[2 * h][1]] += piece
+                odd_ref[placed[2 * h + 1][1]] += piece
         live = i < live_ref[0]
         tiles = []
         for u in range(slots // 2):
@@ -63,41 +75,43 @@
             tiles.append(jnp.where(low_half, left, right))
         sums = jnp.concatenate(tiles, axis=1)
         sums = jnp.where(live, sums, 0.0).astype(jnp.bfloat16).astype(p_ref.dtype)
-        a = jnp.bitwise_and(aggs_ref[i, 0], AGG_DEV - 1)
         if transpose_lhs:
             contrib = lax.dot_general(p_ref[r], sums, (((0,), (0,)), ((), ())), preferred_element_type=jnp.float32)
         else:
             contrib = jnp.dot(p_ref[r].T, sums, preferred_element_type=jnp.float32)
         o_ref[a] += contrib
-        return carry
 
     lax.fori_loop(0, rows, row, 0)
 
 
-def coarse_rows(fine, ghosts, own, cols, aggs, live_count, base, rows=8, group=2, transpose_lhs=True, interpret=False):
+def coarse_rows(
+    fine, ghosts, own, cols, aggs, live_count, base, half, kept, rows=8, group=2, transpose_lhs=True, interpret=False
+):
     capacity, width, span = fine.shape
     slot_width = 3 * AGG_DEV
     ghost_count = ghosts.shape[0]
-    doubled = jnp.concatenate([ghosts, ghosts], axis=2)
+    doubled = ghosts
     grid_spec = pltpu.PrefetchScalarGridSpec(
         num_scalar_prefetch=4,
         grid=(capacity // rows,),
         in_specs=[
             pl.BlockSpec((rows, width, span), lambda b, *_: (b, 0, 0)),
-            pl.BlockSpec((ghost_count, width, 2 * width), lambda b, *_: (0, 0, 0)),
+            pl.BlockSpec(ghosts.shape, lambda b, *_: (0, 0, 0)),
             pl.BlockSpec((rows, width, width), lambda b, *_: (b, 0, 0)),
         ],
-        out_specs=pl.BlockSpec((AGG_DEV, width, slot_width * width), lambda b, *_: (0, 0, 0)),
+        out_specs=pl.BlockSpec((kept, width, slot_width * width), lambda b, *_: (0, 0, 0)),
         scratch_shapes=[
             pltpu.VMEM((slot_width, width, 2 * width), jnp.float32),
             pltpu.VMEM((slot_width, width, 2 * width), jnp.float32),
         ],
     )
-    kernel = functools.partial(coarse_kernel, group=group, transpose_lhs=transpose_lhs, capacity=capacity)
+    kernel = functools.partial(
+        coarse_kernel, group=group, transpose_lhs=transpose_lhs, capacity=capacity, half=half
+    )
     return pl.pallas_call(
         kernel,
         grid_spec=grid_spec,
-        out_shape=jax.ShapeDtypeStruct((AGG_DEV, width, slot_width * width), jnp.float32),
+        out_shape=jax.ShapeDtypeStruct((kept, width, slot_width * width), jnp.float32),
         compiler_params=pltpu.CompilerParams(dimension_semantics=("arbitrary",)),
         interpret=interpret,
     )(cols, aggs, live_count, base, fine, doubled, own)
@@ -121,9 +135,7 @@
     position = lax.axis_index(("grp", "dom"))
     ghosts = extended(prolongator, ((("grp", "dom"), 0),), capacity)
     base = jnp.reshape((position - 1) * capacity, (1,)).astype(jnp.int32)
-    coarse = coarse_rows(
-        fine_matrix_blocks, ghosts, prolongator, block_columns, block_aggregates, live_counts, base
-    )
+    doubled = jnp.concatenate([ghosts, ghosts], axis=2)
     groups_count = lax.axis_size("grp")
     places = lax.axis_size("dom")
     step_stride = places // groups_count
@@ -132,9 +144,17 @@
         for g in range(groups_count)
         for q in range(places)
     ]
-    rotated = lax.ppermute(coarse.astype(jnp.bfloat16), ("grp", "dom"), pairs)
-    copies = jnp.broadcast_to(rotated[None], (groups_count,) + rotated.shape)
-    result = lax.all_to_all(copies, "grp", 0, 0, tiled=True).astype(jnp.float32)
+    halves = 2
+    kept = AGG_DEV // halves
+    gathered = []
+    for half in range(halves):
+        coarse = coarse_rows(
+            fine_matrix_blocks, doubled, prolongator, block_columns, block_aggregates, live_counts, base, half, kept
+        )
+        rotated = lax.ppermute(coarse.astype(jnp.bfloat16), ("grp", "dom"), pairs)
+        copies = jnp.broadcast_to(rotated[None], (groups_count,) + rotated.shape)
+        gathered.append(lax.all_to_all(copies, "grp", 0, 0, tiled=True))
+    result = jnp.concatenate(gathered, axis=1).astype(jnp.float32)
     return result.reshape((groups_count * AGG_DEV,) + coarse.shape[1:])
 
 

time: 141 us -> 150 us (1.064)
  the two profiles are of different devices: /device:TPU:96 before, /device:TPU:32 now
where the time goes in v4:
time: 150 us; the launch traced here: 149 us
  blocking collectives  47.4 us (32%)
  Pallas kernels  46.8 us (31%)
  starting transfers between devices  28.3 us (19%)
  waiting for transfers between devices  10.7 us (7%)
  other arithmetic  10.7 us (7%)
  local copies, waits for them, and re-layouts  4.24 us (3%)
    all_to_all x1, blocking collectives, local(): gathered.append(lax.all_to_all(copies, 'grp', 0, 0, tiled=True))  47.4 us
    pallas_call x2, Pallas kernels, coarse_rows(): pl.pallas_call(kernel, grid_spec=grid_spec, out_shape=jax.ShapeDtypeStruc...  46.8 us
    all_to_all x1, starting transfers between devices, local(): gathered.append(lax.all_to_all(copies, 'grp', 0, 0, tiled=True))  22.7 us
    ppermute x1, waiting for transfers between devices, extended(): lax.ppermute(lax.slice_in_dim(block, 0, width, axis=dim), axis, backward)  6.77 us
    concatenate x1, other arithmetic, local(): doubled = jnp.concatenate([ghosts, ghosts], axis=2)  4.69 us
    ppermute x1, waiting for transfers between devices, extended(): lax.ppermute(lax.slice_in_dim(block, block.shape[dim] - width, None, axis...  3.9 us
    convert_element_type x1, other arithmetic, local(): result = jnp.concatenate(gathered, axis=1).astype(jnp.float32)  3.7 us
  transfers between devices with their start and end apart: 5, of which 2 were waited for; matrix products, arithmetic and copies ran while one was open for 3% of the time, Pallas kernels for 15%

profile of v4, /device:TPU:32, one launch (start us, length us, event | category | flops | bytes accessed | tf_op | source)
XLA Modules:
  0.0 148.9 jit_solution(9189503114942114413)
XLA Ops:
  0.0 1.9 %collective-permute-start.1 = (bf16[64,64,64]{2,1,0:T(8,128)(2,1)}, bf16[64,64,64]{2,1,0:T(8,128)(2,1)S(1)}, u32[]{:S(2)}, u32[]{:S(2)}) collective-permute-start(bf16[64,64,64]{2,1,0:T(8,128)(2,1)} %p_ref.3), channel_id=1, source_target_pairs={{1,0},{2,1},{3,2},{4,3},{5,4},{6,5},{7,6},{8,7},{9,8},{10,9},{11,1... | collective-permute-start | bytes 1572872 | tf_op jit(solution)/shard_map/ppermute | solution.py:128
  1.9 2.4 %collective-permute-start = (bf16[64,64,64]{2,1,0:T(8,128)(2,1)}, bf16[64,64,64]{2,1,0:T(8,128)(2,1)S(1)}, u32[]{:S(2)}, u32[]{:S(2)}) collective-permute-start(bf16[64,64,64]{2,1,0:T(8,128)(2,1)} %p_ref.3), channel_id=1, source_target_pairs={{0,1},{1,2},{2,3},{3,4},{4,5},{5,6},{6,7},{7,8},{8,9},{9,10},{10,1... | collective-permute-start | bytes 1572872 | tf_op jit(solution)/shard_map/ppermute | solution.py:125
  5.0 1.4 copy.6.cols_ref
  6.4 1.4 copy.7.aggs_ref
  7.8 6.8 %collective-permute-done.1 = bf16[64,64,64]{2,1,0:T(8,128)(2,1)S(1)} collective-permute-done((bf16[64,64,64]{2,1,0:T(8,128)(2,1)}, bf16[64,64,64]{2,1,0:T(8,128)(2,1)S(1)}, u32[]{:S(2)}, u32[]{:S(2)}) %collective-permute-start.1) | collective-permute-done | bytes 524320 | tf_op jit(solution)/shard_map/ppermute | solution.py:128
  14.5 3.9 %collective-permute-done = bf16[64,64,64]{2,1,0:T(8,128)(2,1)S(1)} collective-permute-done((bf16[64,64,64]{2,1,0:T(8,128)(2,1)}, bf16[64,64,64]{2,1,0:T(8,128)(2,1)S(1)}, u32[]{:S(2)}, u32[]{:S(2)}) %collective-permute-start) | collective-permute-done | bytes 524320 | tf_op jit(solution)/shard_map/ppermute | solution.py:125
  18.4 4.7 %maximum_maximum_fusion.g_ref = bf16[192,64,128]{2,1,0:T(8,128)(2,1)} fusion(bf16[64,64,64]{2,1,0:T(8,128)(2,1)S(1)} %collective-permute-done.1, bf16[64,64,64]{2,1,0:T(8,128)(2,1)} %p_ref.3, bf16[64,64,64]{2,1,0:T(8,128)(2,1)S(1)} %collective-permute-done), kind=kLoop, calls=%fused_computation | loop fusion | flops 18874368 | bytes 4718592 | tf_op jit(solution)/shard_map/concatenate | solution.py:138
  23.1 23.9 %shard_map.55 = f32[2,64,768]{2,1,0:T(8,128)} custom-call(s32[64,12]{1,0:T(8,128)} %copy.6.cols_ref, s32[64,12]{1,0:T(8,128)} %copy.7.aggs_ref, s32[1]{0:T(128)S(6)} %copy.10.live_ref, s32[1]{0:T(128)} %bitcast.base_ref, bf16[64,64,768]{2,1,0:T(8,128)(2,1)} %f_ref.3, bf16[192,64,128]{2,1,0:T(8,128)(2,1)} %maximum_maximum_fusion.g_ref, bf16[64,64,64]{2,1,0:T(8,128)(2,1)} %p_ref.3), custom_call_target="tpu_custom_call" | custom-call | tf_op jit(solution)/shard_map/pallas_call | solution.py:111
  47.1 1.0 convert_element_type.13
  48.1 0.7 collective-permute-start.2
  48.8 0.0 collective-permute-done.2
  48.8 1.3 broadcast_in_dim.4
  50.1 22.7 %all-to-all-start = ((bf16[8,2,64,768]{3,2,1,0:T(8,128)(2,1)}), bf16[8,2,64,768]{3,2,1,0:T(8,128)(2,1)S(1)}, u32[]{:S(2)}, u32[]{:S(2)}) async-start(bf16[8,2,64,768]{3,2,1,0:T(8,128)(2,1)} %broadcast_in_dim.4), calls=%async_computation | async-start | bytes 3145728 | tf_op jit(solution)/shard_map/all_to_all | solution.py:156
  72.8 22.9 %shard_map.56 = f32[2,64,768]{2,1,0:T(8,128)} custom-call(s32[64,12]{1,0:T(8,128)} %copy.6.cols_ref, s32[64,12]{1,0:T(8,128)} %copy.7.aggs_ref, s32[1]{0:T(128)S(6)} %copy.10.live_ref, s32[1]{0:T(128)} %bitcast.base_ref, bf16[64,64,768]{2,1,0:T(8,128)(2,1)} %f_ref.3, bf16[192,64,128]{2,1,0:T(8,128)(2,1)} %maximum_maximum_fusion.g_ref, bf16[64,64,64]{2,1,0:T(8,128)(2,1)} %p_ref.3), custom_call_target="tpu_custom_call" | custom-call | tf_op jit(solution)/shard_map/pallas_call | solution.py:111
  95.6 1.0 convert_element_type.14
  96.7 0.7 collective-permute-start.3
  97.3 0.0 collective-permute-done.3
  97.4 0.0 all-to-all-done
  97.4 0.1 broadcast_in_dim.5
  97.5 47.4 %all_to_all.10 = bf16[8,2,64,768]{3,2,1,0:T(8,128)(2,1)S(1)} all-to-all(bf16[8,2,64,768]{3,2,1,0:T(8,128)(2,1)S(1)} %broadcast_in_dim.5), channel_id=1, replica_groups=mesh['grp'=8,'dom'=32] {'grp'}, dimensions={0} | all-to-all | bytes 3145728 | tf_op jit(solution)/shard_map/all_to_all | solution.py:156
  145.0 0.3 pad_maximum_fusion
  145.2 3.7 %bitcast_convert_fusion = f32[32,64,768]{2,1,0:T(8,128)} fusion(bf16[8,4,64,768]{3,2,1,0:T(8,128)(2,1)S(1)} %pad_maximum_fusion), kind=kLoop, calls=%fused_computation.2 | loop fusion | flops 1572864 | bytes 9437184 | tf_op jit(solution)/shard_map/convert_element_type | solution.py:157
Async XLA Ops:
  0.0 14.5 %collective-permute-start.1 = (bf16[64,64,64]{2,1,0:T(8,128)(2,1)}, bf16[64,64,64]{2,1,0:T(8,128)(2,1)S(1)}, u32[]{:S(2)}, u32[]{:S(2)}) collective-permute-start(bf16[64,64,64]{2,1,0:T(8,128)(2,1)} %p_ref.3), channel_id=1, source_target_pairs={{1,0},{2,1},{3,2},{4,3},{5,4},{6,5},{7,6},{8,7},{9,8},{10,9},{11,1... | collective-permute-start | bytes 1572872 | tf_op jit(solution)/shard_map/ppermute | solution.py:128
  1.9 16.5 %collective-permute-start = (bf16[64,64,64]{2,1,0:T(8,128)(2,1)}, bf16[64,64,64]{2,1,0:T(8,128)(2,1)S(1)}, u32[]{:S(2)}, u32[]{:S(2)}) collective-permute-start(bf16[64,64,64]{2,1,0:T(8,128)(2,1)} %p_ref.3), channel_id=1, source_target_pairs={{0,1},{1,2},{2,3},{3,4},{4,5},{5,6},{6,7},{7,8},{8,9},{9,10},{10,1... | collective-permute-start | bytes 1572872 | tf_op jit(solution)/shard_map/ppermute | solution.py:125
  48.1 0.7 collective-permute-start.2
  50.1 47.3 %all-to-all-start = ((bf16[8,2,64,768]{3,2,1,0:T(8,128)(2,1)}), bf16[8,2,64,768]{3,2,1,0:T(8,128)(2,1)S(1)}, u32[]{:S(2)}, u32[]{:S(2)}) async-start(bf16[8,2,64,768]{3,2,1,0:T(8,128)(2,1)} %broadcast_in_dim.4), calls=%async_computation | async-start | bytes 3145728 | tf_op jit(solution)/shard_map/all_to_all | solution.py:156
  96.7 0.7 collective-permute-start.3

commit v5 on v3

--- a/solution.py
+++ b/solution.py
@@ -71,7 +71,8 @@
         o_ref[a] += contrib
         return carry
 
-    lax.fori_loop(0, rows, row, 0)
+    for r in range(rows):
+        row(r, 0)
 
 
 def coarse_rows(fine, ghosts, own, cols, aggs, live_count, base, rows=8, group=2, transpose_lhs=True, interpret=False):

time: 141 us -> 132 us (0.936)
  Pallas kernels: 40.1 us -> 31.1 us
    pallas_call x1, Pallas kernels: 40.1 us -> 31.1 us  [coarse_rows(): pl.pallas_call(kernel, grid_spec=grid_spec, out_shape=jax.ShapeDtypeStruc...]
where the time goes in v5:
time: 132 us; the launch traced here: 131 us
  blocking collectives  71.5 us (54%)
  Pallas kernels  31.1 us (24%)
  waiting for transfers between devices  10.5 us (8%)
  other arithmetic  9.56 us (7%)
  starting transfers between devices  5 us (4%)
  local copies, waits for them, and re-layouts  3.14 us (2%)
    all_to_all x1, blocking collectives, local(): result = lax.all_to_all(copies, 'grp', 0, 0, tiled=True).astype(jnp.float32)  71.5 us
    pallas_call x1, Pallas kernels, coarse_rows(): pl.pallas_call(kernel, grid_spec=grid_spec, out_shape=jax.ShapeDtypeStruc...  31.1 us
    ppermute x1, waiting for transfers between devices, extended(): lax.ppermute(lax.slice_in_dim(block, 0, width, axis=dim), axis, backward)  6.75 us
    concatenate x1, other arithmetic, coarse_rows(): doubled = jnp.concatenate([ghosts, ghosts], axis=2)  4.69 us
    ppermute x1, waiting for transfers between devices, extended(): lax.ppermute(lax.slice_in_dim(block, block.shape[dim] - width, None, axis...  3.72 us
    reshape x1, other arithmetic, local(): return result.reshape((groups_count * AGG_DEV,) + coarse.shape[1:])  3.7 us
    unnamed x2, local copies, waits for them, and re-layouts  2.79 us
  transfers between devices with their start and end apart: 3, of which 2 were waited for; matrix products, arithmetic and copies ran while one was open for 2% of the time, Pallas kernels for 0%

profile of v5, /device:TPU:96, one launch (start us, length us, event | category | flops | bytes accessed | tf_op | source)
XLA Modules:
  0.0 131.4 jit_solution(7466679601972166423)
XLA Ops:
  0.0 1.9 %collective-permute-start.1 = (bf16[64,64,64]{2,1,0:T(8,128)(2,1)}, bf16[64,64,64]{2,1,0:T(8,128)(2,1)S(1)}, u32[]{:S(2)}, u32[]{:S(2)}) collective-permute-start(bf16[64,64,64]{2,1,0:T(8,128)(2,1)} %p_ref.1), channel_id=1, source_target_pairs={{1,0},{2,1},{3,2},{4,3},{5,4},{6,5},{7,6},{8,7},{9,8},{10,9},{11,1... | collective-permute-start | bytes 1572872 | tf_op jit(solution)/shard_map/ppermute | solution.py:115
  1.9 2.4 %collective-permute-start = (bf16[64,64,64]{2,1,0:T(8,128)(2,1)}, bf16[64,64,64]{2,1,0:T(8,128)(2,1)S(1)}, u32[]{:S(2)}, u32[]{:S(2)}) collective-permute-start(bf16[64,64,64]{2,1,0:T(8,128)(2,1)} %p_ref.1), channel_id=1, source_target_pairs={{0,1},{1,2},{2,3},{3,4},{4,5},{5,6},{6,7},{7,8},{8,9},{9,10},{10,1... | collective-permute-start | bytes 1572872 | tf_op jit(solution)/shard_map/ppermute | solution.py:112
  5.0 1.4 %copy.6.cols_ref = s32[64,12]{1,0:T(8,128)} copy(s32[64,12]{0,1:T(8,128)} %param.7) | data formatting | bytes 6144 | tf_op args[2]
  6.4 1.4 %copy.7.aggs_ref = s32[64,12]{1,0:T(8,128)} copy(s32[64,12]{0,1:T(8,128)} %param.8) | data formatting | bytes 6144 | tf_op args[3]
  7.8 6.8 %collective-permute-done.1 = bf16[64,64,64]{2,1,0:T(8,128)(2,1)S(1)} collective-permute-done((bf16[64,64,64]{2,1,0:T(8,128)(2,1)}, bf16[64,64,64]{2,1,0:T(8,128)(2,1)S(1)}, u32[]{:S(2)}, u32[]{:S(2)}) %collective-permute-start.1) | collective-permute-done | bytes 524320 | tf_op jit(solution)/shard_map/ppermute | solution.py:115
  14.5 3.7 %collective-permute-done = bf16[64,64,64]{2,1,0:T(8,128)(2,1)S(1)} collective-permute-done((bf16[64,64,64]{2,1,0:T(8,128)(2,1)}, bf16[64,64,64]{2,1,0:T(8,128)(2,1)S(1)}, u32[]{:S(2)}, u32[]{:S(2)}) %collective-permute-start) | collective-permute-done | bytes 524320 | tf_op jit(solution)/shard_map/ppermute | solution.py:112
  18.2 4.7 %maximum_maximum_fusion.g_ref = bf16[192,64,128]{2,1,0:T(8,128)(2,1)} fusion(bf16[64,64,64]{2,1,0:T(8,128)(2,1)S(1)} %collective-permute-done.1, bf16[64,64,64]{2,1,0:T(8,128)(2,1)} %p_ref.1, bf16[64,64,64]{2,1,0:T(8,128)(2,1)S(1)} %collective-permute-done), kind=kLoop, calls=%fused_computation | loop fusion | flops 18874368 | bytes 4718592 | tf_op jit(solution)/shard_map/concatenate | solution.py:82
  22.9 31.1 %shard_map.55 = f32[4,64,768]{2,1,0:T(8,128)} custom-call(s32[64,12]{1,0:T(8,128)} %copy.6.cols_ref, s32[64,12]{1,0:T(8,128)} %copy.7.aggs_ref, s32[1]{0:T(128)S(6)} %copy.8.live_ref, s32[1]{0:T(128)} %bitcast.base_ref, bf16[64,64,768]{2,1,0:T(8,128)(2,1)} %f_ref.1, bf16[192,64,128]{2,1,0:T(8,128)(2,1)} %maximum_maximum_fusion.g_ref, bf16[64,64,64]{2,1,0:T(8,128)(2,1)} %p_ref.1), custom_call_target="tpu_custom_call" | custom-call | tf_op jit(solution)/shard_map/pallas_call | solution.py:98
  54.0 1.2 convert_element_type.4
  55.2 0.7 collective-permute-start.2
  55.9 0.0 collective-permute-done.2
  55.9 0.4 broadcast_in_dim.2
  56.2 71.5 %all_to_all.5 = bf16[8,4,64,768]{3,2,1,0:T(8,128)(2,1)S(1)} all-to-all(bf16[8,4,64,768]{3,2,1,0:T(8,128)(2,1)S(1)} %broadcast_in_dim.2), channel_id=1, replica_groups=mesh['grp'=8,'dom'=32] {'grp'}, dimensions={0} | all-to-all | bytes 6291456 | tf_op jit(solution)/shard_map/all_to_all | solution.py:138
  127.7 3.7 %bitcast_convert_fusion = f32[32,64,768]{2,1,0:T(8,128)} fusion(bf16[8,4,64,768]{3,2,1,0:T(8,128)(2,1)S(1)} %all_to_all.5), kind=kLoop, calls=%fused_computation.1 | loop fusion | flops 1572864 | bytes 9437184 | tf_op jit(solution)/shard_map/reshape | solution.py:139
Async XLA Ops:
  0.0 14.5 %collective-permute-start.1 = (bf16[64,64,64]{2,1,0:T(8,128)(2,1)}, bf16[64,64,64]{2,1,0:T(8,128)(2,1)S(1)}, u32[]{:S(2)}, u32[]{:S(2)}) collective-permute-start(bf16[64,64,64]{2,1,0:T(8,128)(2,1)} %p_ref.1), channel_id=1, source_target_pairs={{1,0},{2,1},{3,2},{4,3},{5,4},{6,5},{7,6},{8,7},{9,8},{10,9},{11,1... | collective-permute-start | bytes 1572872 | tf_op jit(solution)/shard_map/ppermute | solution.py:115
  1.9 16.3 %collective-permute-start = (bf16[64,64,64]{2,1,0:T(8,128)(2,1)}, bf16[64,64,64]{2,1,0:T(8,128)(2,1)S(1)}, u32[]{:S(2)}, u32[]{:S(2)}) collective-permute-start(bf16[64,64,64]{2,1,0:T(8,128)(2,1)} %p_ref.1), channel_id=1, source_target_pairs={{0,1},{1,2},{2,3},{3,4},{4,5},{5,6},{6,7},{7,8},{8,9},{9,10},{10,1... | collective-permute-start | bytes 1572872 | tf_op jit(solution)/shard_map/ppermute | solution.py:112
  55.2 0.7 collective-permute-start.2

commit v6 on v5

--- a/solution.py
+++ b/solution.py
@@ -9,7 +9,7 @@
 AGG_DEV = 4
 
 
-def coarse_kernel(cols_ref, aggs_ref, live_ref, base_ref, f_ref, g_ref, p_ref, o_ref, even_ref, odd_ref, *, group, transpose_lhs, capacity):
+def coarse_kernel(cols_ref, aggs_ref, live_ref, base_ref, f_ref, g_ref, p_ref, o_ref, even_ref, odd_ref, s_ref, *, group, transpose_lhs, capacity):
     step = pl.program_id(0)
     rows = f_ref.shape[0]
     width = p_ref.shape[1]
@@ -26,8 +26,8 @@
     base = base_ref[0]
 
     def place(r_i, k):
-        c = jnp.clip(cols_ref[r_i, k] - base, 0, ghost_count - 1)
-        t = AGG_DEV * (c // capacity) + jnp.bitwise_and(aggs_ref[r_i, k], AGG_DEV - 1)
+        c = jnp.clip(cols_ref[k, r_i] - base, 0, ghost_count - 1)
+        t = AGG_DEV * (c // capacity) + jnp.bitwise_and(aggs_ref[k, r_i], AGG_DEV - 1)
         return c, t
 
     def row(r, carry):
@@ -63,16 +63,17 @@
             tiles.append(jnp.where(low_half, left, right))
         sums = jnp.concatenate(tiles, axis=1)
         sums = jnp.where(live, sums, 0.0).astype(jnp.bfloat16).astype(p_ref.dtype)
-        a = jnp.bitwise_and(aggs_ref[i, 0], AGG_DEV - 1)
-        if transpose_lhs:
-            contrib = lax.dot_general(p_ref[r], sums, (((0,), (0,)), ((), ())), preferred_element_type=jnp.float32)
-        else:
-            contrib = jnp.dot(p_ref[r].T, sums, preferred_element_type=jnp.float32)
-        o_ref[a] += contrib
+        s_ref[width * r : width * (r + 1), :] = sums
         return carry
 
     for r in range(rows):
         row(r, 0)
+    owners = [jnp.bitwise_and(aggs_ref[0, step * rows + r], AGG_DEV - 1) for r in range(rows)]
+    for a in range(AGG_DEV):
+        spread = jnp.concatenate(
+            [jnp.where(owners[r] == a, p_ref[r], jnp.zeros_like(p_ref[r])) for r in range(rows)], axis=0
+        )
+        o_ref[a] += lax.dot_general(spread, s_ref[...], (((0,), (0,)), ((), ())), preferred_element_type=jnp.float32)
 
 
 def coarse_rows(fine, ghosts, own, cols, aggs, live_count, base, rows=8, group=2, transpose_lhs=True, interpret=False):
@@ -92,6 +93,7 @@
         scratch_shapes=[
             pltpu.VMEM((slot_width, width, 2 * width), jnp.float32),
             pltpu.VMEM((slot_width, width, 2 * width), jnp.float32),
+            pltpu.VMEM((rows * width, span), own.dtype),
         ],
     )
     kernel = functools.partial(coarse_kernel, group=group, transpose_lhs=transpose_lhs, capacity=capacity)
@@ -123,7 +125,7 @@
     ghosts = extended(prolongator, ((("grp", "dom"), 0),), capacity)
     base = jnp.reshape((position - 1) * capacity, (1,)).astype(jnp.int32)
     coarse = coarse_rows(
-        fine_matrix_blocks, ghosts, prolongator, block_columns, block_aggregates, live_counts, base
+        fine_matrix_blocks, ghosts, prolongator, block_columns.T, block_aggregates.T, live_counts, base
     )
     groups_count = lax.axis_size("grp")
     places = lax.axis_size("dom")

time: 132 us -> 125 us (0.947)
  Pallas kernels: 31.1 us -> 24.5 us
  waiting for transfers between devices: 10.5 us -> 13.3 us
  local copies, waits for them, and re-layouts: 3.14 us -> 0.35 us
    pallas_call x1, Pallas kernels: 31.1 us -> 24.5 us  [coarse_rows(): pl.pallas_call(kernel, grid_spec=grid_spec, out_shape=jax.ShapeDtypeStruc...]
    unnamed x2 -> x0, local copies, waits for them, and re-layouts: 2.79 us -> none
    ppermute x1, waiting for transfers between devices: 6.75 us -> 9.54 us  [extended(): lax.ppermute(lax.slice_in_dim(block, 0, width, axis=dim), axis, backward)]
  transfers between devices with their start and end apart: 3 -> 3, of which waited for: 2 -> 2; matrix products, arithmetic and copies ran while one was open for 2% -> 0% of each run, Pallas kernels for 0% -> 0%
where the time goes in v6:
time: 125 us
  blocking collectives  71.5 us (57%)
  Pallas kernels  24.5 us (20%)
  waiting for transfers between devices  13.3 us (11%)
  other arithmetic  9.56 us (8%)
  starting transfers between devices  5 us (4%)
    all_to_all x1, blocking collectives, local(): result = lax.all_to_all(copies, 'grp', 0, 0, tiled=True).astype(jnp.float32)  71.5 us
    pallas_call x1, Pallas kernels, coarse_rows(): pl.pallas_call(kernel, grid_spec=grid_spec, out_shape=jax.ShapeDtypeStruc...  24.5 us
    ppermute x1, waiting for transfers between devices, extended(): lax.ppermute(lax.slice_in_dim(block, 0, width, axis=dim), axis, backward)  9.54 us
    concatenate x1, other arithmetic, coarse_rows(): doubled = jnp.concatenate([ghosts, ghosts], axis=2)  4.69 us
    ppermute x1, waiting for transfers between devices, extended(): lax.ppermute(lax.slice_in_dim(block, block.shape[dim] - width, None, axis...  3.72 us
    reshape x1, other arithmetic, local(): return result.reshape((groups_count * AGG_DEV,) + coarse.shape[1:])  3.7 us
  transfers between devices with their start and end apart: 3, of which 2 were waited for; matrix products, arithmetic and copies ran while one was open for 0% of the time, Pallas kernels for 0%

profile of v6, /device:TPU:96, one launch (start us, length us, event | category | flops | bytes accessed | tf_op | source)
XLA Modules:
  0.0 124.8 jit_solution(10425152198045824386)
XLA Ops:
  0.0 1.9 %collective-permute-start.1 = (bf16[64,64,64]{2,1,0:T(8,128)(2,1)}, bf16[64,64,64]{2,1,0:T(8,128)(2,1)S(1)}, u32[]{:S(2)}, u32[]{:S(2)}) collective-permute-start(bf16[64,64,64]{2,1,0:T(8,128)(2,1)} %p_ref.1), channel_id=1, source_target_pairs={{1,0},{2,1},{3,2},{4,3},{5,4},{6,5},{7,6},{8,7},{9,8},{10,9},{11,1... | collective-permute-start | bytes 1572872 | tf_op jit(solution)/shard_map/ppermute | solution.py:117
  1.9 2.4 %collective-permute-start = (bf16[64,64,64]{2,1,0:T(8,128)(2,1)}, bf16[64,64,64]{2,1,0:T(8,128)(2,1)S(1)}, u32[]{:S(2)}, u32[]{:S(2)}) collective-permute-start(bf16[64,64,64]{2,1,0:T(8,128)(2,1)} %p_ref.1), channel_id=1, source_target_pairs={{0,1},{1,2},{2,3},{3,4},{4,5},{5,6},{6,7},{7,8},{8,9},{9,10},{10,1... | collective-permute-start | bytes 1572872 | tf_op jit(solution)/shard_map/ppermute | solution.py:114
  5.0 9.5 %collective-permute-done.1 = bf16[64,64,64]{2,1,0:T(8,128)(2,1)S(1)} collective-permute-done((bf16[64,64,64]{2,1,0:T(8,128)(2,1)}, bf16[64,64,64]{2,1,0:T(8,128)(2,1)S(1)}, u32[]{:S(2)}, u32[]{:S(2)}) %collective-permute-start.1) | collective-permute-done | bytes 524320 | tf_op jit(solution)/shard_map/ppermute | solution.py:117
  14.5 3.7 %collective-permute-done = bf16[64,64,64]{2,1,0:T(8,128)(2,1)S(1)} collective-permute-done((bf16[64,64,64]{2,1,0:T(8,128)(2,1)}, bf16[64,64,64]{2,1,0:T(8,128)(2,1)S(1)}, u32[]{:S(2)}, u32[]{:S(2)}) %collective-permute-start) | collective-permute-done | bytes 524320 | tf_op jit(solution)/shard_map/ppermute | solution.py:114
  18.2 4.7 %maximum_maximum_fusion.g_ref = bf16[192,64,128]{2,1,0:T(8,128)(2,1)} fusion(bf16[64,64,64]{2,1,0:T(8,128)(2,1)S(1)} %collective-permute-done.1, bf16[64,64,64]{2,1,0:T(8,128)(2,1)} %p_ref.1, bf16[64,64,64]{2,1,0:T(8,128)(2,1)S(1)} %collective-permute-done), kind=kLoop, calls=%fused_computation | loop fusion | flops 18874368 | bytes 4718592 | tf_op jit(solution)/shard_map/concatenate | solution.py:83
  22.9 24.5 %shard_map.55 = f32[4,64,768]{2,1,0:T(8,128)} custom-call(s32[12,64]{1,0:T(8,128)} %bitcast.6, s32[12,64]{1,0:T(8,128)} %bitcast.7, s32[1]{0:T(128)S(6)} %copy.6.live_ref, s32[1]{0:T(128)} %bitcast.2.base_ref, bf16[64,64,768]{2,1,0:T(8,128)(2,1)} %f_ref.1, bf16[192,64,128]{2,1,0:T(8,128)(2,1)} %maximum_maximum_fusion.g_ref, bf16[64,64,64]{2,1,0:T(8,128)(2,1)} %p_ref.1), custom_call_target="tpu_custom_call" | custom-call | tf_op jit(solution)/shard_map/pallas_call | solution.py:100
  47.4 1.2 convert_element_type.4
  48.6 0.7 collective-permute-start.2
  49.3 0.0 collective-permute-done.2
  49.3 0.4 broadcast_in_dim.2
  49.6 71.5 %all_to_all.5 = bf16[8,4,64,768]{3,2,1,0:T(8,128)(2,1)S(1)} all-to-all(bf16[8,4,64,768]{3,2,1,0:T(8,128)(2,1)S(1)} %broadcast_in_dim.2), channel_id=1, replica_groups=mesh['grp'=8,'dom'=32] {'grp'}, dimensions={0} | all-to-all | bytes 6291456 | tf_op jit(solution)/shard_map/all_to_all | solution.py:140
  121.1 3.7 %bitcast_convert_fusion = f32[32,64,768]{2,1,0:T(8,128)} fusion(bf16[8,4,64,768]{3,2,1,0:T(8,128)(2,1)S(1)} %all_to_all.5), kind=kLoop, calls=%fused_computation.1 | loop fusion | flops 1572864 | bytes 9437184 | tf_op jit(solution)/shard_map/reshape | solution.py:141
Async XLA Ops:
  0.0 14.5 %collective-permute-start.1 = (bf16[64,64,64]{2,1,0:T(8,128)(2,1)}, bf16[64,64,64]{2,1,0:T(8,128)(2,1)S(1)}, u32[]{:S(2)}, u32[]{:S(2)}) collective-permute-start(bf16[64,64,64]{2,1,0:T(8,128)(2,1)} %p_ref.1), channel_id=1, source_target_pairs={{1,0},{2,1},{3,2},{4,3},{5,4},{6,5},{7,6},{8,7},{9,8},{10,9},{11,1... | collective-permute-start | bytes 1572872 | tf_op jit(solution)/shard_map/ppermute | solution.py:117
  1.9 16.3 %collective-permute-start = (bf16[64,64,64]{2,1,0:T(8,128)(2,1)}, bf16[64,64,64]{2,1,0:T(8,128)(2,1)S(1)}, u32[]{:S(2)}, u32[]{:S(2)}) collective-permute-start(bf16[64,64,64]{2,1,0:T(8,128)(2,1)} %p_ref.1), channel_id=1, source_target_pairs={{0,1},{1,2},{2,3},{3,4},{4,5},{5,6},{6,7},{7,8},{8,9},{9,10},{10,1... | collective-permute-start | bytes 1572872 | tf_op jit(solution)/shard_map/ppermute | solution.py:114
  48.6 0.7 collective-permute-start.2

commit v7 on v6

--- a/solution.py
+++ b/solution.py
@@ -9,7 +9,7 @@
 AGG_DEV = 4
 
 
-def coarse_kernel(cols_ref, aggs_ref, live_ref, base_ref, f_ref, g_ref, p_ref, o_ref, even_ref, odd_ref, s_ref, *, group, transpose_lhs, capacity):
+def coarse_kernel(cols_ref, aggs_ref, live_ref, base_ref, f_ref, g_ref, p_ref, o_ref, even_ref, odd_ref, s_ref, acc_ref, *, group, transpose_lhs, capacity):
     step = pl.program_id(0)
     rows = f_ref.shape[0]
     width = p_ref.shape[1]
@@ -19,7 +19,7 @@
 
     @pl.when(step == 0)
     def _():
-        o_ref[...] = jnp.zeros_like(o_ref)
+        acc_ref[...] = jnp.zeros_like(acc_ref)
 
     lane = lax.broadcasted_iota(jnp.int32, (width, 2 * width), 1)
     low_half = lane < width
@@ -39,7 +39,8 @@
             placed = [place(i, k) for k in ks]
             pieces = []
             for m, (c, _) in enumerate(placed):
-                tile = g_ref[c]
+                raw = g_ref[c]
+                tile = jnp.concatenate([raw, raw], axis=1)
                 pieces.append(jnp.where(low_half if m % 2 == 0 else ~low_half, tile, jnp.zeros_like(tile)))
             if group == 2:
                 block = jnp.concatenate(pieces, axis=0)
@@ -73,20 +74,23 @@
         spread = jnp.concatenate(
             [jnp.where(owners[r] == a, p_ref[r], jnp.zeros_like(p_ref[r])) for r in range(rows)], axis=0
         )
-        o_ref[a] += lax.dot_general(spread, s_ref[...], (((0,), (0,)), ((), ())), preferred_element_type=jnp.float32)
+        acc_ref[a] += lax.dot_general(spread, s_ref[...], (((0,), (0,)), ((), ())), preferred_element_type=jnp.float32)
+
+    @pl.when(step == pl.num_programs(0) - 1)
+    def _():
+        o_ref[...] = acc_ref[...].astype(o_ref.dtype)
 
 
 def coarse_rows(fine, ghosts, own, cols, aggs, live_count, base, rows=8, group=2, transpose_lhs=True, interpret=False):
     capacity, width, span = fine.shape
     slot_width = 3 * AGG_DEV
     ghost_count = ghosts.shape[0]
-    doubled = jnp.concatenate([ghosts, ghosts], axis=2)
     grid_spec = pltpu.PrefetchScalarGridSpec(
         num_scalar_prefetch=4,
         grid=(capacity // rows,),
         in_specs=[
             pl.BlockSpec((rows, width, span), lambda b, *_: (b, 0, 0)),
-            pl.BlockSpec((ghost_count, width, 2 * width), lambda b, *_: (0, 0, 0)),
+            pl.BlockSpec(ghosts.shape, lambda b, *_: (0, 0, 0)),
             pl.BlockSpec((rows, width, width), lambda b, *_: (b, 0, 0)),
         ],
         out_specs=pl.BlockSpec((AGG_DEV, width, slot_width * width), lambda b, *_: (0, 0, 0)),
@@ -94,16 +98,17 @@
             pltpu.VMEM((slot_width, width, 2 * width), jnp.float32),
             pltpu.VMEM((slot_width, width, 2 * width), jnp.float32),
             pltpu.VMEM((rows * width, span), own.dtype),
+            pltpu.VMEM((AGG_DEV, width, slot_width * width), jnp.float32),
         ],
     )
     kernel = functools.partial(coarse_kernel, group=group, transpose_lhs=transpose_lhs, capacity=capacity)
     return pl.pallas_call(
         kernel,
         grid_spec=grid_spec,
-        out_shape=jax.ShapeDtypeStruct((AGG_DEV, width, slot_width * width), jnp.float32),
+        out_shape=jax.ShapeDtypeStruct((AGG_DEV, width, slot_width * width), jnp.bfloat16),
         compiler_params=pltpu.CompilerParams(dimension_semantics=("arbitrary",)),
         interpret=interpret,
-    )(cols, aggs, live_count, base, fine, doubled, own)
+    )(cols, aggs, live_count, base, fine, ghosts, own)
 
 
 def extended(block, sides, width):
@@ -135,7 +140,7 @@
         for g in range(groups_count)
         for q in range(places)
     ]
-    rotated = lax.ppermute(coarse.astype(jnp.bfloat16), ("grp", "dom"), pairs)
+    rotated = lax.ppermute(coarse, ("grp", "dom"), pairs)
     copies = jnp.broadcast_to(rotated[None], (groups_count,) + rotated.shape)
     result = lax.all_to_all(copies, "grp", 0, 0, tiled=True).astype(jnp.float32)
     return result.reshape((groups_count * AGG_DEV,) + coarse.shape[1:])

time: 125 us -> 126 us (level)
  Pallas kernels: 24.5 us -> 27.6 us
  other arithmetic: 9.56 us -> 6.75 us
    pallas_call x1, Pallas kernels: 24.5 us -> 27.6 us  [coarse_rows(): pl.pallas_call(kernel, grid_spec=grid_spec, out_shape=jax.ShapeDtypeStruc...]
    concatenate x1, other arithmetic: 4.69 us -> 3.05 us  [extended(): block = jnp.concatenate([low, block, high], axis=dim)]
where the time goes in v7:
time: 126 us; the launch traced here: 125 us
  blocking collectives  70.7 us (56%)
  Pallas kernels  27.6 us (22%)
  waiting for transfers between devices  13.3 us (11%)
  other arithmetic  6.75 us (5%)
  starting transfers between devices  5.96 us (5%)
    all_to_all x1, blocking collectives, local(): result = lax.all_to_all(copies, 'grp', 0, 0, tiled=True).astype(jnp.float32)  70.7 us
    pallas_call x1, Pallas kernels, coarse_rows(): pl.pallas_call(kernel, grid_spec=grid_spec, out_shape=jax.ShapeDtypeStruc...  27.6 us
    ppermute x1, waiting for transfers between devices, extended(): lax.ppermute(lax.slice_in_dim(block, 0, width, axis=dim), axis, backward)  9.54 us
    ppermute x1, waiting for transfers between devices, extended(): lax.ppermute(lax.slice_in_dim(block, block.shape[dim] - width, None, axis...  3.72 us
    reshape x1, other arithmetic, local(): return result.reshape((groups_count * AGG_DEV,) + coarse.shape[1:])  3.7 us
    concatenate x1, other arithmetic, extended(): block = jnp.concatenate([low, block, high], axis=dim)  3.05 us
  transfers between devices with their start and end apart: 3, of which 2 were waited for; matrix products, arithmetic and copies ran while one was open for 0% of the time, Pallas kernels for 0%

profile of v7, /device:TPU:96, one launch (start us, length us, event | category | flops | bytes accessed | tf_op | source)
XLA Modules:
  0.0 125.4 jit_solution(14829812101000091181)
XLA Ops:
  0.0 1.9 %collective-permute-start.1 = (bf16[64,64,64]{2,1,0:T(8,128)(2,1)}, bf16[64,64,64]{2,1,0:T(8,128)(2,1)S(1)}, u32[]{:S(2)}, u32[]{:S(2)}) collective-permute-start(bf16[64,64,64]{2,1,0:T(8,128)(2,1)} %p_ref.1), channel_id=1, source_target_pairs={{1,0},{2,1},{3,2},{4,3},{5,4},{6,5},{7,6},{8,7},{9,8},{10,9},{11,1... | collective-permute-start | bytes 1572872 | tf_op jit(solution)/shard_map/ppermute | solution.py:122
  1.9 2.4 %collective-permute-start = (bf16[64,64,64]{2,1,0:T(8,128)(2,1)}, bf16[64,64,64]{2,1,0:T(8,128)(2,1)S(1)}, u32[]{:S(2)}, u32[]{:S(2)}) collective-permute-start(bf16[64,64,64]{2,1,0:T(8,128)(2,1)} %p_ref.1), channel_id=1, source_target_pairs={{0,1},{1,2},{2,3},{3,4},{4,5},{5,6},{6,7},{7,8},{8,9},{9,10},{10,1... | collective-permute-start | bytes 1572872 | tf_op jit(solution)/shard_map/ppermute | solution.py:119
  5.0 9.5 %collective-permute-done.1 = bf16[64,64,64]{2,1,0:T(8,128)(2,1)S(1)} collective-permute-done((bf16[64,64,64]{2,1,0:T(8,128)(2,1)}, bf16[64,64,64]{2,1,0:T(8,128)(2,1)S(1)}, u32[]{:S(2)}, u32[]{:S(2)}) %collective-permute-start.1) | collective-permute-done | bytes 524320 | tf_op jit(solution)/shard_map/ppermute | solution.py:122
  14.5 3.7 %collective-permute-done = bf16[64,64,64]{2,1,0:T(8,128)(2,1)S(1)} collective-permute-done((bf16[64,64,64]{2,1,0:T(8,128)(2,1)}, bf16[64,64,64]{2,1,0:T(8,128)(2,1)S(1)}, u32[]{:S(2)}, u32[]{:S(2)}) %collective-permute-start) | collective-permute-done | bytes 524320 | tf_op jit(solution)/shard_map/ppermute | solution.py:119
  18.2 3.1 %pad_maximum_fusion.g_ref = bf16[192,64,64]{2,1,0:T(8,128)(2,1)} fusion(bf16[64,64,64]{2,1,0:T(8,128)(2,1)S(1)} %collective-permute-done.1, bf16[64,64,64]{2,1,0:T(8,128)(2,1)} %p_ref.1, bf16[64,64,64]{2,1,0:T(8,128)(2,1)S(1)} %collective-permute-done), kind=kLoop, calls=%fused_computation | loop fusion | flops 1572864 | bytes 3145728 | tf_op jit(solution)/shard_map/concatenate | solution.py:123
  21.3 27.6 %shard_map.55 = bf16[4,64,768]{2,1,0:T(8,128)(2,1)} custom-call(s32[12,64]{1,0:T(8,128)} %bitcast.6, s32[12,64]{1,0:T(8,128)} %bitcast.7, s32[1]{0:T(128)S(6)} %copy.6.live_ref, s32[1]{0:T(128)} %bitcast.2.base_ref, bf16[64,64,768]{2,1,0:T(8,128)(2,1)} %f_ref.1, bf16[192,64,64]{2,1,0:T(8,128)(2,1)} %pad_maximum_fusion.g_ref, bf16[64,64,64]{2,1,0:T(8,128)(2,1)} %p_ref.1), custom_call_target="tpu_custom_call" | custom-call | tf_op jit(solution)/shard_map/pallas_call | solution.py:105
  48.9 1.6 %collective-permute-start.2 = (bf16[4,64,768]{2,1,0:T(8,128)(2,1)}, bf16[4,64,768]{2,1,0:T(8,128)(2,1)S(1)}, u32[]{:S(2)}, u32[]{:S(2)}) collective-permute-start(bf16[4,64,768]{2,1,0:T(8,128)(2,1)} %shard_map.55), channel_id=1, source_target_pairs={{0,0},{1,1},{2,2},{3,3},{4,4},{5,5},{6,6},{7,7},{8,8},{9,9},{10,10... | collective-permute-start | bytes 1179656 | tf_op jit(solution)/shard_map/ppermute | solution.py:143
  50.6 0.0 collective-permute-done.2
  50.6 0.4 broadcast_in_dim.2
  50.9 70.7 %all_to_all.5 = bf16[8,4,64,768]{3,2,1,0:T(8,128)(2,1)S(1)} all-to-all(bf16[8,4,64,768]{3,2,1,0:T(8,128)(2,1)S(1)} %broadcast_in_dim.2), channel_id=1, replica_groups=mesh['grp'=8,'dom'=32] {'grp'}, dimensions={0} | all-to-all | bytes 6291456 | tf_op jit(solution)/shard_map/all_to_all | solution.py:145
  121.7 3.7 %bitcast_convert_fusion = f32[32,64,768]{2,1,0:T(8,128)} fusion(bf16[8,4,64,768]{3,2,1,0:T(8,128)(2,1)S(1)} %all_to_all.5), kind=kLoop, calls=%fused_computation.1 | loop fusion | flops 1572864 | bytes 9437184 | tf_op jit(solution)/shard_map/reshape | solution.py:146
Async XLA Ops:
  0.0 14.5 %collective-permute-start.1 = (bf16[64,64,64]{2,1,0:T(8,128)(2,1)}, bf16[64,64,64]{2,1,0:T(8,128)(2,1)S(1)}, u32[]{:S(2)}, u32[]{:S(2)}) collective-permute-start(bf16[64,64,64]{2,1,0:T(8,128)(2,1)} %p_ref.1), channel_id=1, source_target_pairs={{1,0},{2,1},{3,2},{4,3},{5,4},{6,5},{7,6},{8,7},{9,8},{10,9},{11,1... | collective-permute-start | bytes 1572872 | tf_op jit(solution)/shard_map/ppermute | solution.py:122
  1.9 16.3 %collective-permute-start = (bf16[64,64,64]{2,1,0:T(8,128)(2,1)}, bf16[64,64,64]{2,1,0:T(8,128)(2,1)S(1)}, u32[]{:S(2)}, u32[]{:S(2)}) collective-permute-start(bf16[64,64,64]{2,1,0:T(8,128)(2,1)} %p_ref.1), channel_id=1, source_target_pairs={{0,1},{1,2},{2,3},{3,4},{4,5},{5,6},{6,7},{7,8},{8,9},{9,10},{10,1... | collective-permute-start | bytes 1572872 | tf_op jit(solution)/shard_map/ppermute | solution.py:119
  48.9 1.6 %collective-permute-start.2 = (bf16[4,64,768]{2,1,0:T(8,128)(2,1)}, bf16[4,64,768]{2,1,0:T(8,128)(2,1)S(1)}, u32[]{:S(2)}, u32[]{:S(2)}) collective-permute-start(bf16[4,64,768]{2,1,0:T(8,128)(2,1)} %shard_map.55), channel_id=1, source_target_pairs={{0,0},{1,1},{2,2},{3,3},{4,4},{5,5},{6,6},{7,7},{8,8},{9,9},{10,10... | collective-permute-start | bytes 1179656 | tf_op jit(solution)/shard_map/ppermute | solution.py:143

commit v8 on v7

--- a/solution.py
+++ b/solution.py
@@ -9,12 +9,11 @@
 AGG_DEV = 4
 
 
-def coarse_kernel(cols_ref, aggs_ref, live_ref, base_ref, f_ref, g_ref, p_ref, o_ref, even_ref, odd_ref, s_ref, acc_ref, *, group, transpose_lhs, capacity):
+def coarse_kernel(cols_ref, aggs_ref, live_ref, base_ref, f_ref, g_ref, p_ref, o_ref, tile_ref, s_ref, acc_ref, *, group, transpose_lhs, capacity):
     step = pl.program_id(0)
     rows = f_ref.shape[0]
     width = p_ref.shape[1]
     blocks = f_ref.shape[2] // width
-    slots = even_ref.shape[0]
     ghost_count = g_ref.shape[0]
 
     @pl.when(step == 0)
@@ -32,8 +31,7 @@
 
     def row(r, carry):
         i = step * rows + r
-        even_ref[...] = jnp.zeros_like(even_ref)
-        odd_ref[...] = jnp.zeros_like(odd_ref)
+        tile_ref[...] = jnp.zeros_like(tile_ref)
         for j in range(blocks // group):
             ks = [group * j + m for m in range(group)]
             placed = [place(i, k) for k in ks]
@@ -53,16 +51,15 @@
                 f_ref[r, :, group * width * j : group * width * (j + 1)], block, preferred_element_type=jnp.float32
             )
             for h in range(group // 2):
-                half = part[:, 2 * width * h : 2 * width * (h + 1)]
-                even_ref[placed[2 * h][1]] += half
-                odd_ref[placed[2 * h + 1][1]] += half
+                same = part[:, 2 * width * h : 2 * width * (h + 1)]
+                swapped = pltpu.roll(same, width, 1)
+                for m, first_src, second_src in ((0, same, swapped), (1, swapped, same)):
+                    t = placed[2 * h + m][1]
+                    odd = jnp.bitwise_and(t, 1) == 1
+                    keep = jnp.logical_xor(low_half, odd)
+                    tile_ref[t // 2] += jnp.where(keep, jnp.where(odd, second_src, first_src), 0.0)
         live = i < live_ref[0]
-        tiles = []
-        for u in range(slots // 2):
-            left = even_ref[2 * u] + pltpu.roll(odd_ref[2 * u], width, 1)
-            right = pltpu.roll(even_ref[2 * u + 1], width, 1) + odd_ref[2 * u + 1]
-            tiles.append(jnp.where(low_half, left, right))
-        sums = jnp.concatenate(tiles, axis=1)
+        sums = jnp.concatenate([tile_ref[u] for u in range(tile_ref.shape[0])], axis=1)
         sums = jnp.where(live, sums, 0.0).astype(jnp.bfloat16).astype(p_ref.dtype)
         s_ref[width * r : width * (r + 1), :] = sums
         return carry
@@ -95,8 +92,7 @@
         ],
         out_specs=pl.BlockSpec((AGG_DEV, width, slot_width * width), lambda b, *_: (0, 0, 0)),
         scratch_shapes=[
-            pltpu.VMEM((slot_width, width, 2 * width), jnp.float32),
-            pltpu.VMEM((slot_width, width, 2 * width), jnp.float32),
+            pltpu.VMEM((slot_width // 2, width, 2 * width), jnp.float32),
             pltpu.VMEM((rows * width, span), own.dtype),
             pltpu.VMEM((AGG_DEV, width, slot_width * width), jnp.float32),
         ],

time: 126 us -> 120 us (0.952)
  Pallas kernels: 27.6 us -> 21.9 us
    pallas_call x1, Pallas kernels: 27.6 us -> 21.9 us  [coarse_rows(): pl.pallas_call(kernel, grid_spec=grid_spec, out_shape=jax.ShapeDtypeStruc...]
where the time goes in v8:
time: 120 us
  blocking collectives  70.7 us (59%)
  Pallas kernels  21.9 us (18%)
  waiting for transfers between devices  13.3 us (11%)
  other arithmetic  6.75 us (6%)
  starting transfers between devices  5.96 us (5%)
    all_to_all x1, blocking collectives, local(): result = lax.all_to_all(copies, 'grp', 0, 0, tiled=True).astype(jnp.float32)  70.7 us
    pallas_call x1, Pallas kernels, coarse_rows(): pl.pallas_call(kernel, grid_spec=grid_spec, out_shape=jax.ShapeDtypeStruc...  21.9 us
    ppermute x1, waiting for transfers between devices, extended(): lax.ppermute(lax.slice_in_dim(block, 0, width, axis=dim), axis, backward)  9.54 us
    ppermute x1, waiting for transfers between devices, extended(): lax.ppermute(lax.slice_in_dim(block, block.shape[dim] - width, None, axis...  3.72 us
    reshape x1, other arithmetic, local(): return result.reshape((groups_count * AGG_DEV,) + coarse.shape[1:])  3.7 us
    concatenate x1, other arithmetic, extended(): block = jnp.concatenate([low, block, high], axis=dim)  3.05 us
    ppermute x1, starting transfers between devices, extended(): lax.ppermute(lax.slice_in_dim(block, block.shape[dim] - width, None, axis...  2.41 us
  transfers between devices with their start and end apart: 3, of which 2 were waited for; matrix products, arithmetic and copies ran while one was open for 0% of the time, Pallas kernels for 0%

profile of v8, /device:TPU:96, one launch (start us, length us, event | category | flops | bytes accessed | tf_op | source)
XLA Modules:
  0.0 119.7 jit_solution(9085990748462421317)
XLA Ops:
  0.0 1.9 %collective-permute-start.1 = (bf16[64,64,64]{2,1,0:T(8,128)(2,1)}, bf16[64,64,64]{2,1,0:T(8,128)(2,1)S(1)}, u32[]{:S(2)}, u32[]{:S(2)}) collective-permute-start(bf16[64,64,64]{2,1,0:T(8,128)(2,1)} %p_ref.1), channel_id=1, source_target_pairs={{1,0},{2,1},{3,2},{4,3},{5,4},{6,5},{7,6},{8,7},{9,8},{10,9},{11,1... | collective-permute-start | bytes 1572872 | tf_op jit(solution)/shard_map/ppermute | solution.py:118
  1.9 2.4 %collective-permute-start = (bf16[64,64,64]{2,1,0:T(8,128)(2,1)}, bf16[64,64,64]{2,1,0:T(8,128)(2,1)S(1)}, u32[]{:S(2)}, u32[]{:S(2)}) collective-permute-start(bf16[64,64,64]{2,1,0:T(8,128)(2,1)} %p_ref.1), channel_id=1, source_target_pairs={{0,1},{1,2},{2,3},{3,4},{4,5},{5,6},{6,7},{7,8},{8,9},{9,10},{10,1... | collective-permute-start | bytes 1572872 | tf_op jit(solution)/shard_map/ppermute | solution.py:115
  5.0 9.5 %collective-permute-done.1 = bf16[64,64,64]{2,1,0:T(8,128)(2,1)S(1)} collective-permute-done((bf16[64,64,64]{2,1,0:T(8,128)(2,1)}, bf16[64,64,64]{2,1,0:T(8,128)(2,1)S(1)}, u32[]{:S(2)}, u32[]{:S(2)}) %collective-permute-start.1) | collective-permute-done | bytes 524320 | tf_op jit(solution)/shard_map/ppermute | solution.py:118
  14.5 3.7 %collective-permute-done = bf16[64,64,64]{2,1,0:T(8,128)(2,1)S(1)} collective-permute-done((bf16[64,64,64]{2,1,0:T(8,128)(2,1)}, bf16[64,64,64]{2,1,0:T(8,128)(2,1)S(1)}, u32[]{:S(2)}, u32[]{:S(2)}) %collective-permute-start) | collective-permute-done | bytes 524320 | tf_op jit(solution)/shard_map/ppermute | solution.py:115
  18.2 3.1 %pad_maximum_fusion.g_ref = bf16[192,64,64]{2,1,0:T(8,128)(2,1)} fusion(bf16[64,64,64]{2,1,0:T(8,128)(2,1)S(1)} %collective-permute-done.1, bf16[64,64,64]{2,1,0:T(8,128)(2,1)} %p_ref.1, bf16[64,64,64]{2,1,0:T(8,128)(2,1)S(1)} %collective-permute-done), kind=kLoop, calls=%fused_computation | loop fusion | flops 1572864 | bytes 3145728 | tf_op jit(solution)/shard_map/concatenate | solution.py:119
  21.3 21.9 %shard_map.55 = bf16[4,64,768]{2,1,0:T(8,128)(2,1)} custom-call(s32[12,64]{1,0:T(8,128)} %bitcast.6, s32[12,64]{1,0:T(8,128)} %bitcast.7, s32[1]{0:T(128)S(6)} %copy.6.live_ref, s32[1]{0:T(128)} %bitcast.2.base_ref, bf16[64,64,768]{2,1,0:T(8,128)(2,1)} %f_ref.1, bf16[192,64,64]{2,1,0:T(8,128)(2,1)} %pad_maximum_fusion.g_ref, bf16[64,64,64]{2,1,0:T(8,128)(2,1)} %p_ref.1), custom_call_target="tpu_custom_call" | custom-call | tf_op jit(solution)/shard_map/pallas_call | solution.py:101
  43.2 1.6 %collective-permute-start.2 = (bf16[4,64,768]{2,1,0:T(8,128)(2,1)}, bf16[4,64,768]{2,1,0:T(8,128)(2,1)S(1)}, u32[]{:S(2)}, u32[]{:S(2)}) collective-permute-start(bf16[4,64,768]{2,1,0:T(8,128)(2,1)} %shard_map.55), channel_id=1, source_target_pairs={{0,0},{1,1},{2,2},{3,3},{4,4},{5,5},{6,6},{7,7},{8,8},{9,9},{10,10... | collective-permute-start | bytes 1179656 | tf_op jit(solution)/shard_map/ppermute | solution.py:139
  44.9 0.0 collective-permute-done.2
  44.9 0.4 broadcast_in_dim.2
  45.2 70.7 %all_to_all.5 = bf16[8,4,64,768]{3,2,1,0:T(8,128)(2,1)S(1)} all-to-all(bf16[8,4,64,768]{3,2,1,0:T(8,128)(2,1)S(1)} %broadcast_in_dim.2), channel_id=1, replica_groups=mesh['grp'=8,'dom'=32] {'grp'}, dimensions={0} | all-to-all | bytes 6291456 | tf_op jit(solution)/shard_map/all_to_all | solution.py:141
  116.0 3.7 %bitcast_convert_fusion = f32[32,64,768]{2,1,0:T(8,128)} fusion(bf16[8,4,64,768]{3,2,1,0:T(8,128)(2,1)S(1)} %all_to_all.5), kind=kLoop, calls=%fused_computation.1 | loop fusion | flops 1572864 | bytes 9437184 | tf_op jit(solution)/shard_map/reshape | solution.py:142
Async XLA Ops:
  0.0 14.5 %collective-permute-start.1 = (bf16[64,64,64]{2,1,0:T(8,128)(2,1)}, bf16[64,64,64]{2,1,0:T(8,128)(2,1)S(1)}, u32[]{:S(2)}, u32[]{:S(2)}) collective-permute-start(bf16[64,64,64]{2,1,0:T(8,128)(2,1)} %p_ref.1), channel_id=1, source_target_pairs={{1,0},{2,1},{3,2},{4,3},{5,4},{6,5},{7,6},{8,7},{9,8},{10,9},{11,1... | collective-permute-start | bytes 1572872 | tf_op jit(solution)/shard_map/ppermute | solution.py:118
  1.9 16.3 %collective-permute-start = (bf16[64,64,64]{2,1,0:T(8,128)(2,1)}, bf16[64,64,64]{2,1,0:T(8,128)(2,1)S(1)}, u32[]{:S(2)}, u32[]{:S(2)}) collective-permute-start(bf16[64,64,64]{2,1,0:T(8,128)(2,1)} %p_ref.1), channel_id=1, source_target_pairs={{0,1},{1,2},{2,3},{3,4},{4,5},{5,6},{6,7},{7,8},{8,9},{9,10},{10,1... | collective-permute-start | bytes 1572872 | tf_op jit(solution)/shard_map/ppermute | solution.py:115
  43.2 1.6 %collective-permute-start.2 = (bf16[4,64,768]{2,1,0:T(8,128)(2,1)}, bf16[4,64,768]{2,1,0:T(8,128)(2,1)S(1)}, u32[]{:S(2)}, u32[]{:S(2)}) collective-permute-start(bf16[4,64,768]{2,1,0:T(8,128)(2,1)} %shard_map.55), channel_id=1, source_target_pairs={{0,0},{1,1},{2,2},{3,3},{4,4},{5,5},{6,6},{7,7},{8,8},{9,9},{10,10... | collective-permute-start | bytes 1179656 | tf_op jit(solution)/shard_map/ppermute | solution.py:139

commit v9 on v8

--- a/solution.py
+++ b/solution.py
@@ -37,8 +37,7 @@
             placed = [place(i, k) for k in ks]
             pieces = []
             for m, (c, _) in enumerate(placed):
-                raw = g_ref[c]
-                tile = jnp.concatenate([raw, raw], axis=1)
+                tile = g_ref[c]
                 pieces.append(jnp.where(low_half if m % 2 == 0 else ~low_half, tile, jnp.zeros_like(tile)))
             if group == 2:
                 block = jnp.concatenate(pieces, axis=0)
@@ -78,16 +77,17 @@
         o_ref[...] = acc_ref[...].astype(o_ref.dtype)
 
 
-def coarse_rows(fine, ghosts, own, cols, aggs, live_count, base, rows=8, group=2, transpose_lhs=True, interpret=False):
+def coarse_rows(fine, ghosts, own, cols, aggs, live_count, base, rows=16, group=2, transpose_lhs=True, interpret=False):
     capacity, width, span = fine.shape
     slot_width = 3 * AGG_DEV
     ghost_count = ghosts.shape[0]
+    doubled = jnp.concatenate([ghosts, ghosts], axis=2)
     grid_spec = pltpu.PrefetchScalarGridSpec(
         num_scalar_prefetch=4,
         grid=(capacity // rows,),
         in_specs=[
             pl.BlockSpec((rows, width, span), lambda b, *_: (b, 0, 0)),
-            pl.BlockSpec(ghosts.shape, lambda b, *_: (0, 0, 0)),
+            pl.BlockSpec(doubled.shape, lambda b, *_: (0, 0, 0)),
             pl.BlockSpec((rows, width, width), lambda b, *_: (b, 0, 0)),
         ],
         out_specs=pl.BlockSpec((AGG_DEV, width, slot_width * width), lambda b, *_: (0, 0, 0)),
@@ -104,7 +104,7 @@
         out_shape=jax.ShapeDtypeStruct((AGG_DEV, width, slot_width * width), jnp.bfloat16),
         compiler_params=pltpu.CompilerParams(dimension_semantics=("arbitrary",)),
         interpret=interpret,
-    )(cols, aggs, live_count, base, fine, ghosts, own)
+    )(cols, aggs, live_count, base, fine, doubled, own)
 
 
 def extended(block, sides, width):

time: 120 us -> 122 us (1.017)
  other arithmetic: 6.75 us -> 8.38 us
    concatenate x1, other arithmetic: 3.05 us -> 4.69 us  [coarse_rows(): doubled = jnp.concatenate([ghosts, ghosts], axis=2)]
where the time goes in v9:
time: 122 us; the launch traced here: 121 us
  blocking collectives  70.8 us (58%)
  Pallas kernels  22 us (18%)
  waiting for transfers between devices  13.3 us (11%)
  other arithmetic  8.38 us (7%)
  starting transfers between devices  5.96 us (5%)
    all_to_all x1, blocking collectives, local(): result = lax.all_to_all(copies, 'grp', 0, 0, tiled=True).astype(jnp.float32)  70.8 us
    pallas_call x1, Pallas kernels, coarse_rows(): pl.pallas_call(kernel, grid_spec=grid_spec, out_shape=jax.ShapeDtypeStruc...  22 us
    ppermute x1, waiting for transfers between devices, extended(): lax.ppermute(lax.slice_in_dim(block, 0, width, axis=dim), axis, backward)  9.54 us
    concatenate x1, other arithmetic, coarse_rows(): doubled = jnp.concatenate([ghosts, ghosts], axis=2)  4.69 us
    ppermute x1, waiting for transfers between devices, extended(): lax.ppermute(lax.slice_in_dim(block, block.shape[dim] - width, None, axis...  3.72 us
    reshape x1, other arithmetic, local(): return result.reshape((groups_count * AGG_DEV,) + coarse.shape[1:])  3.7 us
  transfers between devices with their start and end apart: 3, of which 2 were waited for; matrix products, arithmetic and copies ran while one was open for 0% of the time, Pallas kernels for 0%

profile of v9, /device:TPU:96, one launch (start us, length us, event | category | flops | bytes accessed | tf_op | source)
XLA Modules:
  0.0 121.4 jit_solution(15931872516013864989)
XLA Ops:
  0.0 1.9 %collective-permute-start.1 = (bf16[64,64,64]{2,1,0:T(8,128)(2,1)}, bf16[64,64,64]{2,1,0:T(8,128)(2,1)S(1)}, u32[]{:S(2)}, u32[]{:S(2)}) collective-permute-start(bf16[64,64,64]{2,1,0:T(8,128)(2,1)} %p_ref.1), channel_id=1, source_target_pairs={{1,0},{2,1},{3,2},{4,3},{5,4},{6,5},{7,6},{8,7},{9,8},{10,9},{11,1... | collective-permute-start | bytes 1572872 | tf_op jit(solution)/shard_map/ppermute | solution.py:118
  1.9 2.4 %collective-permute-start = (bf16[64,64,64]{2,1,0:T(8,128)(2,1)}, bf16[64,64,64]{2,1,0:T(8,128)(2,1)S(1)}, u32[]{:S(2)}, u32[]{:S(2)}) collective-permute-start(bf16[64,64,64]{2,1,0:T(8,128)(2,1)} %p_ref.1), channel_id=1, source_target_pairs={{0,1},{1,2},{2,3},{3,4},{4,5},{5,6},{6,7},{7,8},{8,9},{9,10},{10,1... | collective-permute-start | bytes 1572872 | tf_op jit(solution)/shard_map/ppermute | solution.py:115
  5.0 9.5 %collective-permute-done.1 = bf16[64,64,64]{2,1,0:T(8,128)(2,1)S(1)} collective-permute-done((bf16[64,64,64]{2,1,0:T(8,128)(2,1)}, bf16[64,64,64]{2,1,0:T(8,128)(2,1)S(1)}, u32[]{:S(2)}, u32[]{:S(2)}) %collective-permute-start.1) | collective-permute-done | bytes 524320 | tf_op jit(solution)/shard_map/ppermute | solution.py:118
  14.5 3.7 %collective-permute-done = bf16[64,64,64]{2,1,0:T(8,128)(2,1)S(1)} collective-permute-done((bf16[64,64,64]{2,1,0:T(8,128)(2,1)}, bf16[64,64,64]{2,1,0:T(8,128)(2,1)S(1)}, u32[]{:S(2)}, u32[]{:S(2)}) %collective-permute-start) | collective-permute-done | bytes 524320 | tf_op jit(solution)/shard_map/ppermute | solution.py:115
  18.2 4.7 %maximum_maximum_fusion.g_ref = bf16[192,64,128]{2,1,0:T(8,128)(2,1)} fusion(bf16[64,64,64]{2,1,0:T(8,128)(2,1)S(1)} %collective-permute-done.1, bf16[64,64,64]{2,1,0:T(8,128)(2,1)} %p_ref.1, bf16[64,64,64]{2,1,0:T(8,128)(2,1)S(1)} %collective-permute-done), kind=kLoop, calls=%fused_computation | loop fusion | flops 18874368 | bytes 4718592 | tf_op jit(solution)/shard_map/concatenate | solution.py:84
  22.9 22.0 %shard_map.55 = bf16[4,64,768]{2,1,0:T(8,128)(2,1)} custom-call(s32[12,64]{1,0:T(8,128)} %bitcast.6, s32[12,64]{1,0:T(8,128)} %bitcast.7, s32[1]{0:T(128)S(6)} %copy.6.live_ref, s32[1]{0:T(128)} %bitcast.2.base_ref, bf16[64,64,768]{2,1,0:T(8,128)(2,1)} %f_ref.1, bf16[192,64,128]{2,1,0:T(8,128)(2,1)} %maximum_maximum_fusion.g_ref, bf16[64,64,64]{2,1,0:T(8,128)(2,1)} %p_ref.1), custom_call_target="tpu_custom_call" | custom-call | tf_op jit(solution)/shard_map/pallas_call | solution.py:101
  44.9 1.6 %collective-permute-start.2 = (bf16[4,64,768]{2,1,0:T(8,128)(2,1)}, bf16[4,64,768]{2,1,0:T(8,128)(2,1)S(1)}, u32[]{:S(2)}, u32[]{:S(2)}) collective-permute-start(bf16[4,64,768]{2,1,0:T(8,128)(2,1)} %shard_map.55), channel_id=1, source_target_pairs={{0,0},{1,1},{2,2},{3,3},{4,4},{5,5},{6,6},{7,7},{8,8},{9,9},{10,10... | collective-permute-start | bytes 1179656 | tf_op jit(solution)/shard_map/ppermute | solution.py:139
  46.6 0.0 collective-permute-done.2
  46.6 0.4 broadcast_in_dim.2
  46.9 70.8 %all_to_all.5 = bf16[8,4,64,768]{3,2,1,0:T(8,128)(2,1)S(1)} all-to-all(bf16[8,4,64,768]{3,2,1,0:T(8,128)(2,1)S(1)} %broadcast_in_dim.2), channel_id=1, replica_groups=mesh['grp'=8,'dom'=32] {'grp'}, dimensions={0} | all-to-all | bytes 6291456 | tf_op jit(solution)/shard_map/all_to_all | solution.py:141
  117.7 3.7 %bitcast_convert_fusion = f32[32,64,768]{2,1,0:T(8,128)} fusion(bf16[8,4,64,768]{3,2,1,0:T(8,128)(2,1)S(1)} %all_to_all.5), kind=kLoop, calls=%fused_computation.1 | loop fusion | flops 1572864 | bytes 9437184 | tf_op jit(solution)/shard_map/reshape | solution.py:142
Async XLA Ops:
  0.0 14.5 %collective-permute-start.1 = (bf16[64,64,64]{2,1,0:T(8,128)(2,1)}, bf16[64,64,64]{2,1,0:T(8,128)(2,1)S(1)}, u32[]{:S(2)}, u32[]{:S(2)}) collective-permute-start(bf16[64,64,64]{2,1,0:T(8,128)(2,1)} %p_ref.1), channel_id=1, source_target_pairs={{1,0},{2,1},{3,2},{4,3},{5,4},{6,5},{7,6},{8,7},{9,8},{10,9},{11,1... | collective-permute-start | bytes 1572872 | tf_op jit(solution)/shard_map/ppermute | solution.py:118
  1.9 16.3 %collective-permute-start = (bf16[64,64,64]{2,1,0:T(8,128)(2,1)}, bf16[64,64,64]{2,1,0:T(8,128)(2,1)S(1)}, u32[]{:S(2)}, u32[]{:S(2)}) collective-permute-start(bf16[64,64,64]{2,1,0:T(8,128)(2,1)} %p_ref.1), channel_id=1, source_target_pairs={{0,1},{1,2},{2,3},{3,4},{4,5},{5,6},{6,7},{7,8},{8,9},{9,10},{10,1... | collective-permute-start | bytes 1572872 | tf_op jit(solution)/shard_map/ppermute | solution.py:115
  44.9 1.6 %collective-permute-start.2 = (bf16[4,64,768]{2,1,0:T(8,128)(2,1)}, bf16[4,64,768]{2,1,0:T(8,128)(2,1)S(1)}, u32[]{:S(2)}, u32[]{:S(2)}) collective-permute-start(bf16[4,64,768]{2,1,0:T(8,128)(2,1)} %shard_map.55), channel_id=1, source_target_pairs={{0,0},{1,1},{2,2},{3,3},{4,4},{5,5},{6,6},{7,7},{8,8},{9,9},{10,10... | collective-permute-start | bytes 1179656 | tf_op jit(solution)/shard_map/ppermute | solution.py:139

commit v10 on v9

--- a/solution.py
+++ b/solution.py
@@ -77,7 +77,7 @@
         o_ref[...] = acc_ref[...].astype(o_ref.dtype)
 
 
-def coarse_rows(fine, ghosts, own, cols, aggs, live_count, base, rows=16, group=2, transpose_lhs=True, interpret=False):
+def coarse_rows(fine, ghosts, own, cols, aggs, live_count, base, rows=8, group=2, transpose_lhs=True, interpret=False):
     capacity, width, span = fine.shape
     slot_width = 3 * AGG_DEV
     ghost_count = ghosts.shape[0]

time: 122 us -> 122 us (level)
  no operation moved by 1% of the time
where the time goes in v10:
time: 122 us
  blocking collectives  70.8 us (58%)
  Pallas kernels  22.6 us (19%)
  waiting for transfers between devices  13.3 us (11%)
  other arithmetic  8.38 us (7%)
  starting transfers between devices  5.96 us (5%)
    all_to_all x1, blocking collectives, local(): result = lax.all_to_all(copies, 'grp', 0, 0, tiled=True).astype(jnp.float32)  70.8 us
    pallas_call x1, Pallas kernels, coarse_rows(): pl.pallas_call(kernel, grid_spec=grid_spec, out_shape=jax.ShapeDtypeStruc...  22.6 us
    ppermute x1, waiting for transfers between devices, extended(): lax.ppermute(lax.slice_in_dim(block, 0, width, axis=dim), axis, backward)  9.54 us
    concatenate x1, other arithmetic, coarse_rows(): doubled = jnp.concatenate([ghosts, ghosts], axis=2)  4.69 us
    ppermute x1, waiting for transfers between devices, extended(): lax.ppermute(lax.slice_in_dim(block, block.shape[dim] - width, None, axis...  3.72 us
    reshape x1, other arithmetic, local(): return result.reshape((groups_count * AGG_DEV,) + coarse.shape[1:])  3.7 us
  transfers between devices with their start and end apart: 3, of which 2 were waited for; matrix products, arithmetic and copies ran while one was open for 0% of the time, Pallas kernels for 0%

profile of v10, /device:TPU:96, one launch (start us, length us, event | category | flops | bytes accessed | tf_op | source)
XLA Modules:
  0.0 122.0 jit_solution(14320711943385288208)
XLA Ops:
  0.0 1.9 %collective-permute-start.1 = (bf16[64,64,64]{2,1,0:T(8,128)(2,1)}, bf16[64,64,64]{2,1,0:T(8,128)(2,1)S(1)}, u32[]{:S(2)}, u32[]{:S(2)}) collective-permute-start(bf16[64,64,64]{2,1,0:T(8,128)(2,1)} %p_ref.1), channel_id=1, source_target_pairs={{1,0},{2,1},{3,2},{4,3},{5,4},{6,5},{7,6},{8,7},{9,8},{10,9},{11,1... | collective-permute-start | bytes 1572872 | tf_op jit(solution)/shard_map/ppermute | solution.py:118
  1.9 2.4 %collective-permute-start = (bf16[64,64,64]{2,1,0:T(8,128)(2,1)}, bf16[64,64,64]{2,1,0:T(8,128)(2,1)S(1)}, u32[]{:S(2)}, u32[]{:S(2)}) collective-permute-start(bf16[64,64,64]{2,1,0:T(8,128)(2,1)} %p_ref.1), channel_id=1, source_target_pairs={{0,1},{1,2},{2,3},{3,4},{4,5},{5,6},{6,7},{7,8},{8,9},{9,10},{10,1... | collective-permute-start | bytes 1572872 | tf_op jit(solution)/shard_map/ppermute | solution.py:115
  5.0 9.5 %collective-permute-done.1 = bf16[64,64,64]{2,1,0:T(8,128)(2,1)S(1)} collective-permute-done((bf16[64,64,64]{2,1,0:T(8,128)(2,1)}, bf16[64,64,64]{2,1,0:T(8,128)(2,1)S(1)}, u32[]{:S(2)}, u32[]{:S(2)}) %collective-permute-start.1) | collective-permute-done | bytes 524320 | tf_op jit(solution)/shard_map/ppermute | solution.py:118
  14.5 3.7 %collective-permute-done = bf16[64,64,64]{2,1,0:T(8,128)(2,1)S(1)} collective-permute-done((bf16[64,64,64]{2,1,0:T(8,128)(2,1)}, bf16[64,64,64]{2,1,0:T(8,128)(2,1)S(1)}, u32[]{:S(2)}, u32[]{:S(2)}) %collective-permute-start) | collective-permute-done | bytes 524320 | tf_op jit(solution)/shard_map/ppermute | solution.py:115
  18.2 4.7 %maximum_maximum_fusion.g_ref = bf16[192,64,128]{2,1,0:T(8,128)(2,1)} fusion(bf16[64,64,64]{2,1,0:T(8,128)(2,1)S(1)} %collective-permute-done.1, bf16[64,64,64]{2,1,0:T(8,128)(2,1)} %p_ref.1, bf16[64,64,64]{2,1,0:T(8,128)(2,1)S(1)} %collective-permute-done), kind=kLoop, calls=%fused_computation | loop fusion | flops 18874368 | bytes 4718592 | tf_op jit(solution)/shard_map/concatenate | solution.py:84
  22.9 22.6 %shard_map.55 = bf16[4,64,768]{2,1,0:T(8,128)(2,1)} custom-call(s32[12,64]{1,0:T(8,128)} %bitcast.6, s32[12,64]{1,0:T(8,128)} %bitcast.7, s32[1]{0:T(128)S(6)} %copy.6.live_ref, s32[1]{0:T(128)} %bitcast.2.base_ref, bf16[64,64,768]{2,1,0:T(8,128)(2,1)} %f_ref.1, bf16[192,64,128]{2,1,0:T(8,128)(2,1)} %maximum_maximum_fusion.g_ref, bf16[64,64,64]{2,1,0:T(8,128)(2,1)} %p_ref.1), custom_call_target="tpu_custom_call" | custom-call | tf_op jit(solution)/shard_map/pallas_call | solution.py:101
  45.5 1.6 %collective-permute-start.2 = (bf16[4,64,768]{2,1,0:T(8,128)(2,1)}, bf16[4,64,768]{2,1,0:T(8,128)(2,1)S(1)}, u32[]{:S(2)}, u32[]{:S(2)}) collective-permute-start(bf16[4,64,768]{2,1,0:T(8,128)(2,1)} %shard_map.55), channel_id=1, source_target_pairs={{0,0},{1,1},{2,2},{3,3},{4,4},{5,5},{6,6},{7,7},{8,8},{9,9},{10,10... | collective-permute-start | bytes 1179656 | tf_op jit(solution)/shard_map/ppermute | solution.py:139
  47.2 0.0 collective-permute-done.2
  47.2 0.4 broadcast_in_dim.2
  47.5 70.8 %all_to_all.5 = bf16[8,4,64,768]{3,2,1,0:T(8,128)(2,1)S(1)} all-to-all(bf16[8,4,64,768]{3,2,1,0:T(8,128)(2,1)S(1)} %broadcast_in_dim.2), channel_id=1, replica_groups=mesh['grp'=8,'dom'=32] {'grp'}, dimensions={0} | all-to-all | bytes 6291456 | tf_op jit(solution)/shard_map/all_to_all | solution.py:141
  118.3 3.7 %bitcast_convert_fusion = f32[32,64,768]{2,1,0:T(8,128)} fusion(bf16[8,4,64,768]{3,2,1,0:T(8,128)(2,1)S(1)} %all_to_all.5), kind=kLoop, calls=%fused_computation.1 | loop fusion | flops 1572864 | bytes 9437184 | tf_op jit(solution)/shard_map/reshape | solution.py:142
Async XLA Ops:
  0.0 14.5 %collective-permute-start.1 = (bf16[64,64,64]{2,1,0:T(8,128)(2,1)}, bf16[64,64,64]{2,1,0:T(8,128)(2,1)S(1)}, u32[]{:S(2)}, u32[]{:S(2)}) collective-permute-start(bf16[64,64,64]{2,1,0:T(8,128)(2,1)} %p_ref.1), channel_id=1, source_target_pairs={{1,0},{2,1},{3,2},{4,3},{5,4},{6,5},{7,6},{8,7},{9,8},{10,9},{11,1... | collective-permute-start | bytes 1572872 | tf_op jit(solution)/shard_map/ppermute | solution.py:118
  1.9 16.3 %collective-permute-start = (bf16[64,64,64]{2,1,0:T(8,128)(2,1)}, bf16[64,64,64]{2,1,0:T(8,128)(2,1)S(1)}, u32[]{:S(2)}, u32[]{:S(2)}) collective-permute-start(bf16[64,64,64]{2,1,0:T(8,128)(2,1)} %p_ref.1), channel_id=1, source_target_pairs={{0,1},{1,2},{2,3},{3,4},{4,5},{5,6},{6,7},{7,8},{8,9},{9,10},{10,1... | collective-permute-start | bytes 1572872 | tf_op jit(solution)/shard_map/ppermute | solution.py:115
  45.5 1.6 %collective-permute-start.2 = (bf16[4,64,768]{2,1,0:T(8,128)(2,1)}, bf16[4,64,768]{2,1,0:T(8,128)(2,1)S(1)}, u32[]{:S(2)}, u32[]{:S(2)}) collective-permute-start(bf16[4,64,768]{2,1,0:T(8,128)(2,1)} %shard_map.55), channel_id=1, source_target_pairs={{0,0},{1,1},{2,2},{3,3},{4,4},{5,5},{6,6},{7,7},{8,8},{9,9},{10,10... | collective-permute-start | bytes 1179656 | tf_op jit(solution)/shard_map/ppermute | solution.py:139

commit v11 on v8

--- a/solution.py
+++ b/solution.py
@@ -52,12 +52,12 @@
             )
             for h in range(group // 2):
                 same = part[:, 2 * width * h : 2 * width * (h + 1)]
-                swapped = pltpu.roll(same, width, 1)
-                for m, first_src, second_src in ((0, same, swapped), (1, swapped, same)):
+                for m in range(2):
                     t = placed[2 * h + m][1]
-                    odd = jnp.bitwise_and(t, 1) == 1
-                    keep = jnp.logical_xor(low_half, odd)
-                    tile_ref[t // 2] += jnp.where(keep, jnp.where(odd, second_src, first_src), 0.0)
+                    parity = jnp.bitwise_and(t, 1)
+                    moved = pltpu.roll(same, width * jnp.bitwise_xor(parity, m), 1)
+                    keep = jnp.logical_xor(low_half, parity == 1)
+                    tile_ref[t // 2] += jnp.where(keep, moved, 0.0)
         live = i < live_ref[0]
         sums = jnp.concatenate([tile_ref[u] for u in range(tile_ref.shape[0])], axis=1)
         sums = jnp.where(live, sums, 0.0).astype(jnp.bfloat16).astype(p_ref.dtype)

time: 120 us -> 121 us (level)
  no operation moved by 1% of the time
where the time goes in v11:
time: 121 us; the launch traced here: 120 us
  blocking collectives  70.7 us (58%)
  Pallas kernels  22.5 us (19%)
  waiting for transfers between devices  13.3 us (11%)
  other arithmetic  6.75 us (6%)
  starting transfers between devices  5.96 us (5%)
    all_to_all x1, blocking collectives, local(): result = lax.all_to_all(copies, 'grp', 0, 0, tiled=True).astype(jnp.float32)  70.7 us
    pallas_call x1, Pallas kernels, coarse_rows(): pl.pallas_call(kernel, grid_spec=grid_spec, out_shape=jax.ShapeDtypeStruc...  22.5 us
    ppermute x1, waiting for transfers between devices, extended(): lax.ppermute(lax.slice_in_dim(block, 0, width, axis=dim), axis, backward)  9.54 us
    ppermute x1, waiting for transfers between devices, extended(): lax.ppermute(lax.slice_in_dim(block, block.shape[dim] - width, None, axis...  3.72 us
    reshape x1, other arithmetic, local(): return result.reshape((groups_count * AGG_DEV,) + coarse.shape[1:])  3.7 us
    concatenate x1, other arithmetic, extended(): block = jnp.concatenate([low, block, high], axis=dim)  3.05 us
  transfers between devices with their start and end apart: 3, of which 2 were waited for; matrix products, arithmetic and copies ran while one was open for 0% of the time, Pallas kernels for 0%

profile of v11, /device:TPU:96, one launch (start us, length us, event | category | flops | bytes accessed | tf_op | source)
XLA Modules:
  0.0 120.3 jit_solution(18407084423622747938)
XLA Ops:
  0.0 1.9 %collective-permute-start.1 = (bf16[64,64,64]{2,1,0:T(8,128)(2,1)}, bf16[64,64,64]{2,1,0:T(8,128)(2,1)S(1)}, u32[]{:S(2)}, u32[]{:S(2)}) collective-permute-start(bf16[64,64,64]{2,1,0:T(8,128)(2,1)} %p_ref.1), channel_id=1, source_target_pairs={{1,0},{2,1},{3,2},{4,3},{5,4},{6,5},{7,6},{8,7},{9,8},{10,9},{11,1... | collective-permute-start | bytes 1572872 | tf_op jit(solution)/shard_map/ppermute | solution.py:118
  1.9 2.4 %collective-permute-start = (bf16[64,64,64]{2,1,0:T(8,128)(2,1)}, bf16[64,64,64]{2,1,0:T(8,128)(2,1)S(1)}, u32[]{:S(2)}, u32[]{:S(2)}) collective-permute-start(bf16[64,64,64]{2,1,0:T(8,128)(2,1)} %p_ref.1), channel_id=1, source_target_pairs={{0,1},{1,2},{2,3},{3,4},{4,5},{5,6},{6,7},{7,8},{8,9},{9,10},{10,1... | collective-permute-start | bytes 1572872 | tf_op jit(solution)/shard_map/ppermute | solution.py:115
  5.0 9.5 %collective-permute-done.1 = bf16[64,64,64]{2,1,0:T(8,128)(2,1)S(1)} collective-permute-done((bf16[64,64,64]{2,1,0:T(8,128)(2,1)}, bf16[64,64,64]{2,1,0:T(8,128)(2,1)S(1)}, u32[]{:S(2)}, u32[]{:S(2)}) %collective-permute-start.1) | collective-permute-done | bytes 524320 | tf_op jit(solution)/shard_map/ppermute | solution.py:118
  14.5 3.7 %collective-permute-done = bf16[64,64,64]{2,1,0:T(8,128)(2,1)S(1)} collective-permute-done((bf16[64,64,64]{2,1,0:T(8,128)(2,1)}, bf16[64,64,64]{2,1,0:T(8,128)(2,1)S(1)}, u32[]{:S(2)}, u32[]{:S(2)}) %collective-permute-start) | collective-permute-done | bytes 524320 | tf_op jit(solution)/shard_map/ppermute | solution.py:115
  18.2 3.1 %pad_maximum_fusion.g_ref = bf16[192,64,64]{2,1,0:T(8,128)(2,1)} fusion(bf16[64,64,64]{2,1,0:T(8,128)(2,1)S(1)} %collective-permute-done.1, bf16[64,64,64]{2,1,0:T(8,128)(2,1)} %p_ref.1, bf16[64,64,64]{2,1,0:T(8,128)(2,1)S(1)} %collective-permute-done), kind=kLoop, calls=%fused_computation | loop fusion | flops 1572864 | bytes 3145728 | tf_op jit(solution)/shard_map/concatenate | solution.py:119
  21.3 22.5 %shard_map.55 = bf16[4,64,768]{2,1,0:T(8,128)(2,1)} custom-call(s32[12,64]{1,0:T(8,128)} %bitcast.6, s32[12,64]{1,0:T(8,128)} %bitcast.7, s32[1]{0:T(128)S(6)} %copy.6.live_ref, s32[1]{0:T(128)} %bitcast.2.base_ref, bf16[64,64,768]{2,1,0:T(8,128)(2,1)} %f_ref.1, bf16[192,64,64]{2,1,0:T(8,128)(2,1)} %pad_maximum_fusion.g_ref, bf16[64,64,64]{2,1,0:T(8,128)(2,1)} %p_ref.1), custom_call_target="tpu_custom_call" | custom-call | tf_op jit(solution)/shard_map/pallas_call | solution.py:101
  43.8 1.6 %collective-permute-start.2 = (bf16[4,64,768]{2,1,0:T(8,128)(2,1)}, bf16[4,64,768]{2,1,0:T(8,128)(2,1)S(1)}, u32[]{:S(2)}, u32[]{:S(2)}) collective-permute-start(bf16[4,64,768]{2,1,0:T(8,128)(2,1)} %shard_map.55), channel_id=1, source_target_pairs={{0,0},{1,1},{2,2},{3,3},{4,4},{5,5},{6,6},{7,7},{8,8},{9,9},{10,10... | collective-permute-start | bytes 1179656 | tf_op jit(solution)/shard_map/ppermute | solution.py:139
  45.5 0.0 collective-permute-done.2
  45.5 0.4 broadcast_in_dim.2
  45.8 70.7 %all_to_all.5 = bf16[8,4,64,768]{3,2,1,0:T(8,128)(2,1)S(1)} all-to-all(bf16[8,4,64,768]{3,2,1,0:T(8,128)(2,1)S(1)} %broadcast_in_dim.2), channel_id=1, replica_groups=mesh['grp'=8,'dom'=32] {'grp'}, dimensions={0} | all-to-all | bytes 6291456 | tf_op jit(solution)/shard_map/all_to_all | solution.py:141
  116.6 3.7 %bitcast_convert_fusion = f32[32,64,768]{2,1,0:T(8,128)} fusion(bf16[8,4,64,768]{3,2,1,0:T(8,128)(2,1)S(1)} %all_to_all.5), kind=kLoop, calls=%fused_computation.1 | loop fusion | flops 1572864 | bytes 9437184 | tf_op jit(solution)/shard_map/reshape | solution.py:142
Async XLA Ops:
  0.0 14.5 %collective-permute-start.1 = (bf16[64,64,64]{2,1,0:T(8,128)(2,1)}, bf16[64,64,64]{2,1,0:T(8,128)(2,1)S(1)}, u32[]{:S(2)}, u32[]{:S(2)}) collective-permute-start(bf16[64,64,64]{2,1,0:T(8,128)(2,1)} %p_ref.1), channel_id=1, source_target_pairs={{1,0},{2,1},{3,2},{4,3},{5,4},{6,5},{7,6},{8,7},{9,8},{10,9},{11,1... | collective-permute-start | bytes 1572872 | tf_op jit(solution)/shard_map/ppermute | solution.py:118
  1.9 16.3 %collective-permute-start = (bf16[64,64,64]{2,1,0:T(8,128)(2,1)}, bf16[64,64,64]{2,1,0:T(8,128)(2,1)S(1)}, u32[]{:S(2)}, u32[]{:S(2)}) collective-permute-start(bf16[64,64,64]{2,1,0:T(8,128)(2,1)} %p_ref.1), channel_id=1, source_target_pairs={{0,1},{1,2},{2,3},{3,4},{4,5},{5,6},{6,7},{7,8},{8,9},{9,10},{10,1... | collective-permute-start | bytes 1572872 | tf_op jit(solution)/shard_map/ppermute | solution.py:115
  43.8 1.6 %collective-permute-start.2 = (bf16[4,64,768]{2,1,0:T(8,128)(2,1)}, bf16[4,64,768]{2,1,0:T(8,128)(2,1)S(1)}, u32[]{:S(2)}, u32[]{:S(2)}) collective-permute-start(bf16[4,64,768]{2,1,0:T(8,128)(2,1)} %shard_map.55), channel_id=1, source_target_pairs={{0,0},{1,1},{2,2},{3,3},{4,4},{5,5},{6,6},{7,7},{8,8},{9,9},{10,10... | collective-permute-start | bytes 1179656 | tf_op jit(solution)/shard_map/ppermute | solution.py:139
